TPU v7x, 512 devices: a whole 4x4x16 slice. The times are simulated.
512 devices in a mesh: tiles: 32 (over z, core), chan: 16 (over y, x).
Axes of the slice: x: 4, y: 4, z: 16, core: 2. Of those that a mesh axis runs over, the one named last changes fastest.
Arguments:
- atmos_state: bfloat16 [256, 192, 256], P('tiles', 'chan'), may hold values from -6 to 6
- ocean_state: bfloat16 [256, 128, 256], P('tiles', 'chan'), may hold values from -6 to 6
- atmos_weight: bfloat16 [9, 192, 192], P(None, 'chan'), may hold values from -0.15625 to 0.15625
- ocean_weight: bfloat16 [9, 128, 128], P(None, 'chan'), may hold values from -0.1875 to 0.1875
- couple_weight: bfloat16 [128, 192], P('chan'), may hold values from -0.4375 to 0.4375
- sea_mask: int32 [256], replicated, may hold values from 0 to 1, as said below
- neighbours: int32 [256, 4], replicated, may hold values from 0 to 255, as said below
- rotations: int32 [256, 4], replicated, may hold values from 0 to 7
Outputs:
- atmos_next: bfloat16 [256, 192, 256], P('tiles', 'chan')
- ocean_next: bfloat16 [192, 128, 256], P('tiles', 'chan')
Inputs may be any that keep to these rules, and one draw needn't show every extreme that they name: `sea_mask`: exactly 192 of the 256 entries are 1; the tiles of blocks 2k and 2k + 1 of 8 tiles hold exactly 12 sea tiles together, and each such block holds between 4 and 8. neighbours[t, s] lies in the block of 8 tiles that holds t, or in the block just before or just after it, cyclically over the 32 blocks.
All inputs are finite; a program needn't handle non-finite values.
Results may differ from a plain program's by a relative error of at most 0.0034.
Values may be sent and summed in bfloat16 or wider, within the bound.
No kernel may reach another device: no remote copies, remote signals or barrier semaphores. Data moves between devices by JAX's collectives and lax.ppermute only.
A program may use at most 64 MiB of HBM per device.

v0:
```python
import jax
import jax.numpy as jnp
from jax import lax
from jax.sharding import PartitionSpec as P

SIDE = 16


def padded_2(cells, sides, width):
    for axis, dim in sides:
        count = lax.axis_size(axis)
        head = lax.slice_in_dim(cells, 0, width, axis=dim)
        tail = lax.slice_in_dim(cells, cells.shape[dim] - width, cells.shape[dim], axis=dim)
        cells = jnp.concatenate(
            [
                lax.ppermute(tail, axis, [(i, (i + 1) % count) for i in range(count)]),
                cells,
                lax.ppermute(head, axis, [((i + 1) % count, i) for i in range(count)]),
            ],
            axis=dim,
        )
    return cells


def partner(value, axis, distance):
    mask = 2**distance
    pairs = [(source, source ^ mask) for source in range(lax.axis_size(axis))]
    return lax.ppermute(value, axis, pairs)


def edge_set(tile_field):
    tile_count, chan_count = (tile_field.shape[0], tile_field.shape[1])
    tile_grid = tile_field.reshape(tile_count, chan_count, SIDE, SIDE)
    return jnp.stack(
        [
            tile_grid[:, :, 0, :],
            tile_grid[:, :, :, SIDE - 1],
            tile_grid[:, :, SIDE - 1, :],
            tile_grid[:, :, :, 0],
        ],
        axis=2,
    )


def pick_rims(edge_strips, adjacent, turn_codes):
    picked = edge_strips[adjacent]
    side_index = turn_codes % 4
    chosen = picked[:, :, :, 0, :]
    for edge_id in range(1, 4):
        chosen = jnp.where(
            (side_index == edge_id)[:, :, None, None], picked[:, :, :, edge_id, :], chosen
        )
    return jnp.where((turn_codes >= 4)[:, :, None, None], chosen[..., ::-1], chosen)


def pad_tile(tile_field, rim_cells):
    tile_count, chan_count = (tile_field.shape[0], tile_field.shape[1])
    tile_grid = tile_field.reshape(tile_count, chan_count, SIDE, SIDE)
    upper_row = jnp.pad(rim_cells[:, 0], ((0, 0), (0, 0), (1, 1)))[:, :, None, :]
    bottom = jnp.pad(rim_cells[:, 2], ((0, 0), (0, 0), (1, 1)))[:, :, None, :]
    middle = jnp.concatenate(
        [rim_cells[:, 3][:, :, :, None], tile_grid, rim_cells[:, 1][:, :, :, None]], axis=3
    )
    assembled = jnp.concatenate([upper_row, middle, bottom], axis=2).reshape(
        tile_count, chan_count, (SIDE + 2) * (SIDE + 2)
    )
    return jnp.pad(assembled, ((0, 0), (0, 0), (0, 2)))


def trim_columns(accum):
    tile_count, chan_count = (accum.shape[0], accum.shape[1])
    return accum.reshape(tile_count, chan_count, SIDE, SIDE + 2)[:, :, :, :SIDE].reshape(
        tile_count, chan_count, SIDE * SIDE
    )


def conv_step(weight, accum, piece):
    row_width = SIDE + 2
    out_span = SIDE * row_width
    for tap_index in range(9):
        offset = tap_index // 3 * row_width + tap_index % 3
        accum = accum + jnp.einsum(
            "oc,bcp->bop",
            weight[tap_index],
            piece[:, :, offset : offset + out_span],
            preferred_element_type=jnp.float32,
        )
    return accum


def ocean_layer(padded, forcing, own_state, ocean_weight, couple_weight):
    tile_count = padded.shape[0]
    out_chans = ocean_weight.shape[1]
    conv_start = jnp.zeros((tile_count, out_chans, SIDE * (SIDE + 2)), jnp.float32)
    conv_accum = conv_step(
        ocean_weight, conv_start, lax.all_gather(padded, "chan", axis=1, tiled=True)
    )
    couple_accum = jnp.einsum(
        "oc,bcp->bop",
        couple_weight,
        lax.all_gather(forcing, "chan", axis=1, tiled=True),
        preferred_element_type=jnp.float32,
    )
    mixed = trim_columns(conv_accum) + couple_accum
    return (own_state.astype(jnp.float32) + jax.nn.gelu(mixed, approximate=True)).astype(
        jnp.bfloat16
    )


def local(
    atmos_state,
    ocean_state,
    atmos_weight,
    ocean_weight,
    couple_weight,
    sea_mask,
    neighbours,
    rotations,
):
    per_dev = atmos_state.shape[0]
    atmos_local = atmos_state.shape[1]
    ocean_local = ocean_state.shape[1]
    groups = lax.axis_size("tiles")
    tile_group = lax.axis_index("tiles")
    first_tile = tile_group * per_dev
    sea_here = lax.dynamic_slice_in_dim(sea_mask, first_tile, per_dev, 0)
    sea_field = ocean_state * sea_here.astype(jnp.bfloat16)[:, None, None]
    edge_strips = jnp.concatenate([edge_set(atmos_state), edge_set(sea_field)], axis=1)
    widened = padded_2(edge_strips.reshape(per_dev, -1), (("tiles", 0),), per_dev)
    widened = widened.reshape(3 * per_dev, atmos_local + ocean_local, 4, SIDE)
    adjacent = lax.dynamic_slice_in_dim(neighbours, first_tile, per_dev, 0)
    turn_codes = lax.dynamic_slice_in_dim(rotations, first_tile, per_dev, 0)
    local_adjacent = (adjacent // per_dev - tile_group + 1) % groups * per_dev + adjacent % per_dev
    rim_cells = pick_rims(widened, local_adjacent, turn_codes)
    atmos_pad = pad_tile(atmos_state, rim_cells[:, :, :atmos_local])
    atmos_start = jnp.zeros((per_dev, atmos_weight.shape[1], SIDE * (SIDE + 2)), jnp.float32)
    atmos_accum = conv_step(
        atmos_weight, atmos_start, lax.all_gather(atmos_pad, "chan", axis=1, tiled=True)
    )
    atmos_next = (
        atmos_state.astype(jnp.float32) + jax.nn.gelu(trim_columns(atmos_accum), approximate=True)
    ).astype(jnp.bfloat16)
    per_owner = per_dev * 3 // 4
    ocean_total = per_owner * groups
    counts = jnp.sum(sea_mask.reshape(groups, per_dev), axis=1)
    starts = jnp.cumsum(counts) - counts
    sea_rank = jnp.cumsum(sea_mask) - 1
    rank_spots = jnp.where(sea_mask == 1, sea_rank, ocean_total)
    tile_of_rank = (
        jnp.zeros((ocean_total,), jnp.int32)
        .at[rank_spots]
        .set(jnp.arange(sea_mask.shape[0], dtype=jnp.int32), mode="drop")
    )
    my_first = starts[tile_group]
    my_last = my_first + counts[tile_group]
    parity = tile_group % 2
    pair_base = tile_group // 2 * 2 * per_owner
    slot_ids = jnp.arange(per_owner, dtype=jnp.int32)
    ranks_send = pair_base + 2 * slot_ids + (1 - parity)
    ranks_own = pair_base + 2 * slot_ids + parity
    send_tile = jnp.clip(tile_of_rank[ranks_send] - first_tile, 0, per_dev - 1)
    own_tile = jnp.clip(tile_of_rank[ranks_own] - first_tile, 0, per_dev - 1)
    from_here = (ranks_own >= my_first) & (ranks_own < my_last)
    block_width = (ocean_local + atmos_local) * SIDE * SIDE
    sea_block = jnp.concatenate([ocean_state, atmos_next], axis=1).reshape(per_dev, block_width)
    rim_flat = rim_cells[:, :, atmos_local:].reshape(per_dev, -1)
    packed = jnp.concatenate([sea_block, rim_flat], axis=1)
    received = partner(packed[send_tile], "tiles", 0)
    own_packed = jnp.where(from_here[:, None], packed[own_tile], received)
    own_block = own_packed[:, :block_width].reshape(
        per_owner, ocean_local + atmos_local, SIDE * SIDE
    )
    own_rims = own_packed[:, block_width:].reshape(per_owner, 4, ocean_local, SIDE)
    own_state = own_block[:, :ocean_local]
    ocean_next = ocean_layer(
        pad_tile(own_state, own_rims),
        own_block[:, ocean_local:],
        own_state,
        ocean_weight,
        couple_weight,
    )
    return (atmos_next, ocean_next)


def solution(mesh):
    placed = (
        P("tiles", "chan", None),
        P("tiles", "chan", None),
        P(None, "chan", None),
        P(None, "chan", None),
        P("chan", None),
        P(),
        P(),
        P(),
    )
    return jax.shard_map(
        local,
        mesh=mesh,
        in_specs=placed,
        out_specs=(P("tiles", "chan", None), P("tiles", "chan", None)),
        check_vma=False,
    )
```

profile of v0, /device:TPU:6, one launch (start us, length us, event | category | flops | bytes accessed | tf_op | source)
XLA Modules:
  0.0 114.3 jit_solution(959433694621876811)
XLA Ops:
  0.7 0.8 dynamic-slice_convert_fusion
  1.4 0.8 broadcast_multiply_fusion
  2.7 1.1 copy.100
  5.6 8.9 %collective-permute-start.1 = (bf16[8,1280]{1,0:T(8,128)(2,1)S(1)}, bf16[8,1280]{1,0:T(8,128)(2,1)S(1)}, u32[]{:S(2)}, u32[]{:S(2)}) collective-permute-start(bf16[8,1280]{1,0:T(8,128)(2,1)S(1)} %reshape.192), channel_id=1, source_target_pairs={{16,0},{32,16},{48,32},{64,48},{80,64},{96,80},{112,96},{128,112},... | collective-permute-start | bytes 61448 | tf_op jit(solution)/shard_map/ppermute | solution.py:18
  15.6 1.4 %scatter_custom_fusion = s32[192]{0:T(256)S(1)} fusion(s32[256]{0:T(256)S(1)} %compare_select_fusion.1, s32[256]{0:T(256)S(1)} %iota.13, s32[]{:T(128)} %constant.105.clone.1), kind=kCustom, calls=%fused_computation.181 | custom fusion | bytes 772 | tf_op jit(solution)/shard_map/scatter | solution.py:152
  17.0 0.6 gather_fusion.1
  17.6 0.6 gather_fusion.3
  18.5 0.6 dynamic_slice.19
  19.4 0.6 dynamic_slice.18
  22.4 0.6 gather_fusion
  24.0 0.5 pad_maximum_fusion
  24.5 1.6 %copy.122 = bf16[8,12,18,18]{3,2,0,1:T(8,128)(2,1)S(1)} copy(bf16[8,12,18,18]{1,3,2,0:T(8,128)(2,1)S(1)} %pad_maximum_fusion) | data formatting | bytes 124416 | tf_op jit(solution)/shard_map/concatenate | solution.py:64
  26.4 25.0 %all_gather.9 = bf16[8,192,326]{2,0,1:T(8,128)(2,1)S(1)} all-gather(bf16[8,12,326]{2,0,1:T(8,128)(2,1)S(1)} %pad.24), channel_id=1, replica_groups=mesh['tiles'=32,'chan'=16] {'chan'}, dimensions={1}, use_global_device_ids=true | all-gather | bytes 1064064 | tf_op jit(solution)/shard_map/all_gather | solution.py:138
  51.4 3.0 %fusion.131 = (bf16[8,192,288]{2,0,1:T(8,128)(2,1)S(1)}, bf16[8,192,288]{2,0,1:T(8,128)(2,1)S(1)}, bf16[8,192,288]{2,0,1:T(8,128)(2,1)S(1)}, bf16[8,192,288]{2,0...) fusion(bf16[8,192,326]{2,0,1:T(8,128)(2,1)S(1)} %all_gather.9), kind=kLoop, calls=%fused_computation.184 | loop fusion | bytes 15925248 | tf_op jit(solution)/shard_map/slice | solution.py:85
  56.9 0.5 reshape.194
  57.8 0.6 gather_fusion.4
  58.4 2.1 %collective-permute-start.2 = (bf16[6,5632]{1,0:T(8,128)(2,1)S(1)}, bf16[6,5632]{1,0:T(8,128)(2,1)S(1)}, u32[]{:S(2)}, u32[]{:S(2)}) collective-permute-start(bf16[6,5632]{1,0:T(8,128)(2,1)S(1)} %gather_fusion.4), channel_id=1, source_target_pairs={{0,16},{16,0},{32,48},{48,32},{64,80},{80,64},{96,112},{112,96},{1... | collective-permute-start | bytes 202760 | tf_op jit(solution)/shard_map/ppermute | solution.py:28
  60.6 0.7 compare_and_fusion
  61.2 0.6 gather_fusion.2
  62.6 0.4 copy.140
  63.4 0.4 pad_maximum_fusion.2
  64.0 22.6 %all_gather.10 = bf16[6,128,326]{2,1,0:T(8,128)(2,1)S(1)} all-gather(bf16[6,8,326]{2,1,0:T(8,128)(2,1)S(1)} %pad.27), channel_id=1, replica_groups=mesh['tiles'=32,'chan'=16] {'chan'}, dimensions={1}, use_global_device_ids=true | all-gather | bytes 532032 | tf_op jit(solution)/shard_map/all_gather | solution.py:96
  90.1 23.3 %all_gather.11 = bf16[6,192,256]{2,0,1:T(8,128)(2,1)S(1)} all-gather(bf16[6,12,256]{2,0,1:T(8,128)(2,1)S(1)} %copy.153), channel_id=1, replica_groups=mesh['tiles'=32,'chan'=16] {'chan'}, dimensions={1}, use_global_device_ids=true | all-gather | bytes 626688 | tf_op jit(solution)/shard_map/all_gather | solution.py:101
  113.4 0.8 add_convert_fusion
  (124 shorter events, 13.5 us)
Async XLA Ops:
  0.6 112.8 %copy-start = (bf16[8,192]{1,0:T(8,128)(2,1)S(1)}, bf16[8,192]{1,0:T(8,128)(2,1)}, u32[]{:S(2)}) copy-start(bf16[8,192]{1,0:T(8,128)(2,1)} %param.12) | copy-start | bytes 9220
  2.7 11.9 %copy-start.5 = (s32[256]{0:T(256)S(1)}, s32[256]{0:T(256)}, u32[]{:S(2)}) copy-start(s32[256]{0:T(256)} %param.13) | copy-start | bytes 3076
  2.7 12.5 %copy-start.6 = (s32[256,4]{0,1:T(4,128)S(1)}, s32[256,4]{0,1:T(4,128)}, u32[]{:S(2)}) copy-start(s32[256,4]{0,1:T(4,128)} %param.14) | copy-start | bytes 12292
  2.7 12.7 %copy-start.7 = (s32[256,4]{0,1:T(4,128)S(1)}, s32[256,4]{0,1:T(4,128)}, u32[]{:S(2)}) copy-start(s32[256,4]{0,1:T(4,128)} %param.15) | copy-start | bytes 12292
  4.4 14.0 %copy-start.3 = (bf16[8,8,256]{2,1,0:T(8,128)(2,1)S(1)}, bf16[8,8,256]{2,1,0:T(8,128)(2,1)}, u32[]{:S(2)}) copy-start(bf16[8,8,256]{2,1,0:T(8,128)(2,1)} %param.9) | copy-start | bytes 98308
  5.6 16.2 %collective-permute-start.1 = (bf16[8,1280]{1,0:T(8,128)(2,1)S(1)}, bf16[8,1280]{1,0:T(8,128)(2,1)S(1)}, u32[]{:S(2)}, u32[]{:S(2)}) collective-permute-start(bf16[8,1280]{1,0:T(8,128)(2,1)S(1)} %reshape.192), channel_id=1, source_target_pairs={{16,0},{32,16},{48,32},{64,48},{80,64},{96,80},{112,96},{128,112},... | collective-permute-start | bytes 61448 | tf_op jit(solution)/shard_map/ppermute | solution.py:18
  14.5 6.8 %collective-permute-start = (bf16[8,1280]{1,0:T(8,128)(2,1)S(1)}, bf16[8,1280]{1,0:T(8,128)(2,1)S(1)}, u32[]{:S(2)}, u32[]{:S(2)}) collective-permute-start(bf16[8,1280]{1,0:T(8,128)(2,1)S(1)} %reshape.192), channel_id=1, source_target_pairs={{0,16},{16,32},{32,48},{48,64},{64,80},{80,96},{96,112},{112,128},... | collective-permute-start | bytes 61448 | tf_op jit(solution)/shard_map/ppermute | solution.py:16
  51.4 3.0 %copy-start.8 = (bf16[9,12,192]{2,1,0:T(8,128)(2,1)S(1)}, bf16[9,12,192]{2,1,0:T(8,128)(2,1)}, u32[]{:S(2)}) copy-start(bf16[9,12,192]{2,1,0:T(8,128)(2,1)} %param.10) | copy-start | bytes 124420
  56.8 0.9 copy-start.1
  57.8 4.1 %copy-start.2 = (bf16[8,12,256]{2,0,1:T(8,128)(2,1)}, bf16[8,12,256]{2,0,1:T(8,128)(2,1)S(1)}, u32[]{:S(2)}) copy-start(bf16[8,12,256]{2,0,1:T(8,128)(2,1)S(1)} %fusion.69) | copy-start | bytes 147460
  58.4 3.4 %collective-permute-start.2 = (bf16[6,5632]{1,0:T(8,128)(2,1)S(1)}, bf16[6,5632]{1,0:T(8,128)(2,1)S(1)}, u32[]{:S(2)}, u32[]{:S(2)}) collective-permute-start(bf16[6,5632]{1,0:T(8,128)(2,1)S(1)} %gather_fusion.4), channel_id=1, source_target_pairs={{0,16},{16,0},{32,48},{48,32},{64,80},{80,64},{96,112},{112,96},{1... | collective-permute-start | bytes 202760 | tf_op jit(solution)/shard_map/ppermute | solution.py:28
  62.6 24.0 %copy-start.4 = (bf16[9,8,128]{2,1,0:T(8,128)(2,1)S(1)}, bf16[9,8,128]{2,1,0:T(8,128)(2,1)}, u32[]{:S(2)}) copy-start(bf16[9,8,128]{2,1,0:T(8,128)(2,1)} %param.11) | copy-start | bytes 55300
where the time goes:
time: 115 us; the launch traced here: 114 us
  blocking collectives  70.9 us (62%)
  local copies, waits for them, and re-layouts  18.7 us (16%)
  starting transfers between devices  11.1 us (10%)
  matrix products  6.31 us (5%)
  other arithmetic  4.8 us (4%)
  between operations  2.53 us (2%)
    all_gather x1, blocking collectives, local(): lax.all_gather(atmos_pad, 'chan', axis=1, tiled=True)  25 us
    all_gather x1, blocking collectives, ocean_layer(): lax.all_gather(forcing, 'chan', axis=1, tiled=True)  23.3 us
    all_gather x1, blocking collectives, ocean_layer(): lax.all_gather(padded, 'chan', axis=1, tiled=True)  22.6 us
    ppermute x1, starting transfers between devices, padded_2(): lax.ppermute(head, axis, [((i + 1) % count, i) for i in range(count)])  8.95 us
    dot_general x18, matrix products, conv_step(): jnp.einsum('oc,bcp->bop', weight[tap_index], piece[:, :, offset:offset +...  5.48 us
    slice x1, local copies, waits for them, and re-layouts, conv_step(): piece[:, :, offset:offset + out_span]  2.97 us
  transfers between devices with their start and end apart: 3, of which 0 were waited for; matrix products, arithmetic and copies ran while one was open for 6% of the time, Pallas kernels for 0%

commit v1 on v0

--- a/solution.py
+++ b/solution.py
@@ -88,23 +88,26 @@
     return accum
 
 
-def ocean_layer(padded, forcing, own_state, ocean_weight, couple_weight):
-    tile_count = padded.shape[0]
-    out_chans = ocean_weight.shape[1]
-    conv_start = jnp.zeros((tile_count, out_chans, SIDE * (SIDE + 2)), jnp.float32)
-    conv_accum = conv_step(
-        ocean_weight, conv_start, lax.all_gather(padded, "chan", axis=1, tiled=True)
-    )
-    couple_accum = jnp.einsum(
-        "oc,bcp->bop",
-        couple_weight,
-        lax.all_gather(forcing, "chan", axis=1, tiled=True),
-        preferred_element_type=jnp.float32,
-    )
-    mixed = trim_columns(conv_accum) + couple_accum
-    return (own_state.astype(jnp.float32) + jax.nn.gelu(mixed, approximate=True)).astype(
-        jnp.bfloat16
-    )
+def gather_rows(pieces):
+    flat = jnp.concatenate([piece.reshape(-1) for piece in pieces])
+    rows = flat.reshape(-1, SIDE * SIDE)
+    gathered = lax.all_gather(rows, "chan", axis=0, tiled=False)
+    groups = gathered.shape[0]
+    gathered = gathered.reshape(groups, -1)
+    parts = []
+    offset = 0
+    for piece in pieces:
+        size = piece.size
+        part = gathered[:, offset : offset + size].reshape((groups,) + piece.shape)
+        parts.append(part)
+        offset += size
+    return parts
+
+
+def merge_chans(part, chan_dim):
+    moved = jnp.moveaxis(part, 0, chan_dim)
+    shape = moved.shape
+    return moved.reshape(shape[:chan_dim] + (shape[chan_dim] * shape[chan_dim + 1],) + shape[chan_dim + 2 :])
 
 
 def local(
@@ -123,23 +126,6 @@
     groups = lax.axis_size("tiles")
     tile_group = lax.axis_index("tiles")
     first_tile = tile_group * per_dev
-    sea_here = lax.dynamic_slice_in_dim(sea_mask, first_tile, per_dev, 0)
-    sea_field = ocean_state * sea_here.astype(jnp.bfloat16)[:, None, None]
-    edge_strips = jnp.concatenate([edge_set(atmos_state), edge_set(sea_field)], axis=1)
-    widened = padded_2(edge_strips.reshape(per_dev, -1), (("tiles", 0),), per_dev)
-    widened = widened.reshape(3 * per_dev, atmos_local + ocean_local, 4, SIDE)
-    adjacent = lax.dynamic_slice_in_dim(neighbours, first_tile, per_dev, 0)
-    turn_codes = lax.dynamic_slice_in_dim(rotations, first_tile, per_dev, 0)
-    local_adjacent = (adjacent // per_dev - tile_group + 1) % groups * per_dev + adjacent % per_dev
-    rim_cells = pick_rims(widened, local_adjacent, turn_codes)
-    atmos_pad = pad_tile(atmos_state, rim_cells[:, :, :atmos_local])
-    atmos_start = jnp.zeros((per_dev, atmos_weight.shape[1], SIDE * (SIDE + 2)), jnp.float32)
-    atmos_accum = conv_step(
-        atmos_weight, atmos_start, lax.all_gather(atmos_pad, "chan", axis=1, tiled=True)
-    )
-    atmos_next = (
-        atmos_state.astype(jnp.float32) + jax.nn.gelu(trim_columns(atmos_accum), approximate=True)
-    ).astype(jnp.bfloat16)
     per_owner = per_dev * 3 // 4
     ocean_total = per_owner * groups
     counts = jnp.sum(sea_mask.reshape(groups, per_dev), axis=1)
@@ -161,23 +147,54 @@
     send_tile = jnp.clip(tile_of_rank[ranks_send] - first_tile, 0, per_dev - 1)
     own_tile = jnp.clip(tile_of_rank[ranks_own] - first_tile, 0, per_dev - 1)
     from_here = (ranks_own >= my_first) & (ranks_own < my_last)
-    block_width = (ocean_local + atmos_local) * SIDE * SIDE
-    sea_block = jnp.concatenate([ocean_state, atmos_next], axis=1).reshape(per_dev, block_width)
-    rim_flat = rim_cells[:, :, atmos_local:].reshape(per_dev, -1)
-    packed = jnp.concatenate([sea_block, rim_flat], axis=1)
-    received = partner(packed[send_tile], "tiles", 0)
-    own_packed = jnp.where(from_here[:, None], packed[own_tile], received)
-    own_block = own_packed[:, :block_width].reshape(
-        per_owner, ocean_local + atmos_local, SIDE * SIDE
-    )
-    own_rims = own_packed[:, block_width:].reshape(per_owner, 4, ocean_local, SIDE)
-    own_state = own_block[:, :ocean_local]
-    ocean_next = ocean_layer(
-        pad_tile(own_state, own_rims),
-        own_block[:, ocean_local:],
-        own_state,
-        ocean_weight,
-        couple_weight,
+
+    own_ocean = jnp.where(
+        from_here[:, None, None], ocean_state[own_tile], partner(ocean_state[send_tile], "tiles", 0)
+    )
+
+    sea_here = lax.dynamic_slice_in_dim(sea_mask, first_tile, per_dev, 0)
+    sea_field = ocean_state * sea_here.astype(jnp.bfloat16)[:, None, None]
+    edge_strips = jnp.concatenate([edge_set(atmos_state), edge_set(sea_field)], axis=1)
+    widened = padded_2(edge_strips.reshape(per_dev, -1), (("tiles", 0),), per_dev)
+    widened = widened.reshape(3 * per_dev, atmos_local + ocean_local, 4, SIDE)
+    adjacent = lax.dynamic_slice_in_dim(neighbours, first_tile, per_dev, 0)
+    turn_codes = lax.dynamic_slice_in_dim(rotations, first_tile, per_dev, 0)
+    local_adjacent = (adjacent // per_dev - tile_group + 1) % groups * per_dev + adjacent % per_dev
+    rim_cells = pick_rims(widened, local_adjacent, turn_codes)
+
+    early = 2 * SIDE
+    atmos_int, atmos_rims, ocean_head = gather_rows(
+        [atmos_state, rim_cells[:, :, :atmos_local], own_ocean[:, :, :early]]
+    )
+    atmos_pad = pad_tile(merge_chans(atmos_int, 1), merge_chans(atmos_rims, 2))
+    atmos_start = jnp.zeros((per_dev, atmos_weight.shape[1], SIDE * (SIDE + 2)), jnp.float32)
+    atmos_accum = conv_step(atmos_weight, atmos_start, atmos_pad)
+    atmos_next = (
+        atmos_state.astype(jnp.float32) + jax.nn.gelu(trim_columns(atmos_accum), approximate=True)
+    ).astype(jnp.bfloat16)
+
+    sea_width = ocean_local * 4 * SIDE
+    late_block = jnp.concatenate(
+        [atmos_next.reshape(per_dev, -1), rim_cells[:, :, atmos_local:].reshape(per_dev, -1)], axis=1
+    )
+    late_own = jnp.where(
+        from_here[:, None], late_block[own_tile], partner(late_block[send_tile], "tiles", 0)
+    )
+    forcing = late_own[:, : late_block.shape[1] - sea_width].reshape(per_owner, atmos_local, SIDE * SIDE)
+    own_rims = late_own[:, late_block.shape[1] - sea_width :].reshape(per_owner, 4, ocean_local, SIDE)
+
+    ocean_tail, ocean_rims, force_parts = gather_rows([own_ocean[:, :, early:], own_rims, forcing])
+    ocean_full = jnp.concatenate([merge_chans(ocean_head, 1), merge_chans(ocean_tail, 1)], axis=2)
+    ocean_pad = pad_tile(ocean_full, merge_chans(ocean_rims, 2))
+    force_all = merge_chans(force_parts, 1)
+    conv_start = jnp.zeros((per_owner, ocean_weight.shape[1], SIDE * (SIDE + 2)), jnp.float32)
+    conv_accum = conv_step(ocean_weight, conv_start, ocean_pad)
+    couple_accum = jnp.einsum(
+        "oc,bcp->bop", couple_weight, force_all, preferred_element_type=jnp.float32
+    )
+    mixed = trim_columns(conv_accum) + couple_accum
+    ocean_next = (own_ocean.astype(jnp.float32) + jax.nn.gelu(mixed, approximate=True)).astype(
+        jnp.bfloat16
     )
     return (atmos_next, ocean_next)
 

time: 115 us -> 153 us (1.33)
  local copies, waits for them, and re-layouts: 18.7 us -> 62.6 us
  blocking collectives: 70.9 us -> 47.7 us
  other arithmetic: 4.8 us -> 17.2 us
  matrix products: 6.31 us -> 8.22 us
  starting transfers between devices: 11.1 us -> 12.8 us
    all_gather x3 -> x2, blocking collectives: 70.9 us -> 47.7 us  [gather_rows(): gathered = lax.all_gather(rows, 'chan', axis=0, tiled=False)]
    concatenate x2 -> x5, other arithmetic: 0.02 us -> 12.6 us  [the longest x1 12.4 us: pad_tile(): jnp.concatenate([rim_cells[:, 3][:, :, :, None], tile_grid, rim_cells[:,...]
    concatenate x1 -> x2, local copies, waits for them, and re-layouts: 1.59 us -> 12.1 us  [the longest x1 11.9 us: pad_tile(): jnp.concatenate([rim_cells[:, 3][:, :, :, None], tile_grid, rim_cells[:,...]
    reshape x4 -> x16, local copies, waits for them, and re-layouts: 0.5 us -> 9.04 us  [the longest x6 4.72 us: gather_rows(): part = gathered[:, offset:offset + size].reshape((groups,) + piece.shape)]
    another operation x2 -> x7, local copies, waits for them, and re-layouts: 0.2 us -> 6.23 us  [the longest x1 5.88 us: pad_tile(): tile_grid = tile_field.reshape(tile_count, chan_count, SIDE, SIDE)]
    transpose x0 -> x3, local copies, waits for them, and re-layouts: none -> 5.42 us  [merge_chans(): moved = jnp.moveaxis(part, 0, chan_dim)]
    another operation x2, local copies, waits for them, and re-layouts: 0.44 us -> 5.8 us  [pad_tile(): rim_cells[:, 1][:, :, :, None]]
    another operation x2, local copies, waits for them, and re-layouts: 0.44 us -> 5.76 us  [pad_tile(): rim_cells[:, 3][:, :, :, None]]
  transfers between devices with their start and end apart: 3 -> 4, of which waited for: 0 -> 1; matrix products, arithmetic and copies ran while one was open for 6% -> 8% of each run, Pallas kernels for 0% -> 0%
where the time goes in v1:
time: 153 us; the launch traced here: 152 us
  local copies, waits for them, and re-layouts  62.6 us (41%)
  blocking collectives  47.7 us (31%)
  other arithmetic  17.2 us (11%)
  starting transfers between devices  12.8 us (8%)
  matrix products  8.22 us (5%)
  between operations  2.66 us (2%)
    all_gather x2, blocking collectives, gather_rows(): gathered = lax.all_gather(rows, 'chan', axis=0, tiled=False)  47.7 us
    concatenate x1, other arithmetic, pad_tile(): jnp.concatenate([rim_cells[:, 3][:, :, :, None], tile_grid, rim_cells[:,...  12.4 us
    concatenate x1, local copies, waits for them, and re-layouts, pad_tile(): jnp.concatenate([rim_cells[:, 3][:, :, :, None], tile_grid, rim_cells[:,...  11.9 us
    ppermute x1, starting transfers between devices, padded_2(): lax.ppermute(head, axis, [((i + 1) % count, i) for i in range(count)])  8.95 us
    dot_general x18, matrix products, conv_step(): jnp.einsum('oc,bcp->bop', weight[tap_index], piece[:, :, offset:offset +...  7.4 us
    another operation x1, local copies, waits for them, and re-layouts, pad_tile(): tile_grid = tile_field.reshape(tile_count, chan_count, SIDE, SIDE)  5.88 us
    another operation x2, local copies, waits for them, and re-layouts, pad_tile(): rim_cells[:, 1][:, :, :, None]  5.8 us
    another operation x2, local copies, waits for them, and re-layouts, pad_tile(): rim_cells[:, 3][:, :, :, None]  5.76 us
  transfers between devices with their start and end apart: 4, of which 1 were waited for; matrix products, arithmetic and copies ran while one was open for 8% of the time, Pallas kernels for 0%

profile of v1, /device:TPU:6, one launch (start us, length us, event | category | flops | bytes accessed | tf_op | source)
XLA Modules:
  0.0 151.6 jit_solution(7309678719529264888)
XLA Ops:
  0.7 0.8 dynamic-slice_convert_fusion
  1.4 0.8 broadcast_multiply_fusion
  2.7 1.1 copy.182
  5.5 8.9 %collective-permute-start.1 = (bf16[8,1280]{1,0:T(8,128)(2,1)S(1)}, bf16[8,1280]{1,0:T(8,128)(2,1)S(1)}, u32[]{:S(2)}, u32[]{:S(2)}) collective-permute-start(bf16[8,1280]{1,0:T(8,128)(2,1)S(1)} %reshape.246), channel_id=1, source_target_pairs={{16,0},{32,16},{48,32},{64,48},{80,64},{96,80},{112,96},{128,112},... | collective-permute-start | bytes 61448 | tf_op jit(solution)/shard_map/ppermute | solution.py:18
  15.1 1.4 scatter_custom_fusion
  16.5 0.6 gather_fusion.3
  17.7 1.9 %collective-permute-start.2 = (bf16[6,8,256]{2,1,0:T(8,128)(2,1)S(1)}, bf16[6,8,256]{2,1,0:T(8,128)(2,1)S(1)}, u32[]{:S(2)}, u32[]{:S(2)}) collective-permute-start(bf16[6,8,256]{2,1,0:T(8,128)(2,1)S(1)} %gather_fusion.4), channel_id=1, source_target_pairs={{0,16},{16,0},{32,48},{48,32},{64,80},{80,64},{96,112},{112,96},{1... | collective-permute-start | bytes 73736 | tf_op jit(solution)/shard_map/ppermute | solution.py:28
  20.2 0.6 gather_fusion.1
  23.7 0.7 compare_and_fusion
  26.5 0.6 gather_fusion
  29.4 24.7 %all_gather.6 = bf16[16,126,256]{2,1,0:T(8,128)(2,1)S(1)} all-gather(bf16[1,126,256]{2,1,0:T(8,128)(2,1)S(1)} %all_gather_reshape.6), channel_id=1, replica_groups=mesh['tiles'=32,'chan'=16] {'chan'}, dimensions={0}, use_global_device_ids=true | all-gather | bytes 1096704 | tf_op jit(solution)/shard_map/all_gather | solution.py:94
  54.8 0.6 reshape.257
  55.8 2.3 %reshape.255 = bf16[16,8,4,12,16]{4,3,2,1,0:T(8,128)(2,1)S(1)} reshape(bf16[16,6144]{1,0:T(8,128)(2,1)S(1)} %slice.331) | data formatting | bytes 393216 | tf_op jit(solution)/shard_map/reshape | solution.py:101
  58.1 5.0 %copy.203 = bf16[8,4,16,12,16]{3,2,4,1,0:T(8,128)(2,1)} copy(bf16[8,4,16,12,16]{4,3,1,0,2:T(8,128)(2,1)S(1)} %bitcast.197) | data formatting | bytes 393216 | tf_op jit(solution)/shard_map/transpose | solution.py:108
  63.2 3.4 %reshape.256 = bf16[8,4,192,16]{2,3,1,0:T(8,128)(2,1)S(1)} reshape(bf16[8,4,16,12,16]{3,2,4,1,0:T(8,128)(2,1)} %copy.203) | data formatting | bytes 393216 | tf_op jit(solution)/shard_map/reshape | solution.py:110
  66.7 5.9 %reshape_reshape.9 = bf16[8,192,16,16]{3,2,0,1:T(8,128)(2,1)} reshape(bf16[8,16,12,256]{3,0,2,1:T(8,128)(2,1)S(1)} %copy.204) | data formatting | bytes 1572864 | tf_op jit(solution)/shard_map/reshape;reshape | solution.py:58
  72.6 5.6 %copy.206 = bf16[8,192,16,1]{3,2,0,1:T(8,128)(2,1)} copy(bf16[8,192,16,1]{1,2,0,3:T(8,128)(2,1)S(1)} %get-tuple-element.22) | data formatting | bytes 98304 | tf_op jit(solution)/shard_map/broadcast_in_dim;squeeze | solution.py:62
  78.2 5.6 %copy.205 = bf16[8,192,16,1]{3,2,0,1:T(8,128)(2,1)} copy(bf16[8,192,16,1]{1,2,0,3:T(8,128)(2,1)S(1)} %get-tuple-element.23) | data formatting | bytes 98304 | tf_op jit(solution)/shard_map/broadcast_in_dim;squeeze | solution.py:62
  83.8 12.4 %pad_maximum_fusion = bf16[8,192,16,18]{3,2,0,1:T(8,128)(2,1)} fusion(bf16[8,192,16,1]{3,2,0,1:T(8,128)(2,1)} %copy.206, bf16[8,192,16,16]{3,2,0,1:T(8,128)(2,1)} %reshape_reshape.9, bf16[8,192,16,1]{3,2,0,1:T(8,128)(2,1)} %copy.205), kind=kLoop, calls=%fused_computation.8 | loop fusion | flops 2654208 | bytes 1769472 | tf_op jit(solution)/shard_map/concatenate | solution.py:61
  96.2 11.9 %copy.209 = bf16[8,192,16,18]{1,0,3,2:T(8,128)(2,1)S(1)} copy(bf16[8,192,16,18]{3,2,0,1:T(8,128)(2,1)} %pad_maximum_fusion) | data formatting | bytes 1769472 | tf_op jit(solution)/shard_map/concatenate | solution.py:61
  108.4 1.5 copy.210
  116.3 1.9 %collective-permute-start.3 = (bf16[6,3584]{1,0:T(8,128)(2,1)S(1)}, bf16[6,3584]{1,0:T(8,128)(2,1)S(1)}, u32[]{:S(2)}, u32[]{:S(2)}) collective-permute-start(bf16[6,3584]{1,0:T(8,128)(2,1)S(1)} %gather_fusion.6), channel_id=1, source_target_pairs={{0,16},{16,0},{32,48},{48,32},{64,80},{80,64},{96,112},{112,96},{1... | collective-permute-start | bytes 129032 | tf_op jit(solution)/shard_map/ppermute | solution.py:28
  119.7 23.0 %all_gather.7 = bf16[16,126,256]{2,1,0:T(8,128)(2,1)S(1)} all-gather(bf16[1,126,256]{2,1,0:T(8,128)(2,1)S(1)} %all_gather_reshape.7), channel_id=1, replica_groups=mesh['tiles'=32,'chan'=16] {'chan'}, dimensions={0}, use_global_device_ids=true | all-gather | bytes 1096704 | tf_op jit(solution)/shard_map/all_gather | solution.py:94
  150.7 0.8 add_convert_fusion
  (167 shorter events, 26.6 us)
Async XLA Ops:
  0.6 150.1 %copy-start = (bf16[8,192]{1,0:T(8,128)(2,1)S(1)}, bf16[8,192]{1,0:T(8,128)(2,1)}, u32[]{:S(2)}) copy-start(bf16[8,192]{1,0:T(8,128)(2,1)} %param.12) | copy-start | bytes 9220
  2.6 11.8 %copy-start.4 = (s32[256]{0:T(256)S(1)}, s32[256]{0:T(256)}, u32[]{:S(2)}) copy-start(s32[256]{0:T(256)} %param.13) | copy-start | bytes 3076
  3.8 13.4 %copy-start.2 = (bf16[8,8,256]{2,1,0:T(8,128)(2,1)S(1)}, bf16[8,8,256]{2,1,0:T(8,128)(2,1)}, u32[]{:S(2)}) copy-start(bf16[8,8,256]{2,1,0:T(8,128)(2,1)} %param.9) | copy-start | bytes 98308
  3.8 16.0 %copy-start.6 = (s32[256,4]{0,1:T(4,128)S(1)}, s32[256,4]{0,1:T(4,128)}, u32[]{:S(2)}) copy-start(s32[256,4]{0,1:T(4,128)} %param.14) | copy-start | bytes 12292
  3.8 16.2 %copy-start.7 = (s32[256,4]{0,1:T(4,128)S(1)}, s32[256,4]{0,1:T(4,128)}, u32[]{:S(2)}) copy-start(s32[256,4]{0,1:T(4,128)} %param.15) | copy-start | bytes 12292
  4.6 19.7 %copy-start.1 = (bf16[8,12,256]{2,0,1:T(8,128)(2,1)S(1)}, bf16[8,12,256]{2,0,1:T(8,128)(2,1)}, u32[]{:S(2)}) copy-start(bf16[8,12,256]{2,0,1:T(8,128)(2,1)} %param.8) | copy-start | bytes 147460
  5.5 20.3 %collective-permute-start.1 = (bf16[8,1280]{1,0:T(8,128)(2,1)S(1)}, bf16[8,1280]{1,0:T(8,128)(2,1)S(1)}, u32[]{:S(2)}, u32[]{:S(2)}) collective-permute-start(bf16[8,1280]{1,0:T(8,128)(2,1)S(1)} %reshape.246), channel_id=1, source_target_pairs={{16,0},{32,16},{48,32},{64,48},{80,64},{96,80},{112,96},{128,112},... | collective-permute-start | bytes 61448 | tf_op jit(solution)/shard_map/ppermute | solution.py:18
  14.5 10.9 %collective-permute-start = (bf16[8,1280]{1,0:T(8,128)(2,1)S(1)}, bf16[8,1280]{1,0:T(8,128)(2,1)S(1)}, u32[]{:S(2)}, u32[]{:S(2)}) collective-permute-start(bf16[8,1280]{1,0:T(8,128)(2,1)S(1)} %reshape.246), channel_id=1, source_target_pairs={{0,16},{16,32},{32,48},{48,64},{64,80},{80,96},{96,112},{112,128},... | collective-permute-start | bytes 61448 | tf_op jit(solution)/shard_map/ppermute | solution.py:16
  17.7 11.5 %collective-permute-start.2 = (bf16[6,8,256]{2,1,0:T(8,128)(2,1)S(1)}, bf16[6,8,256]{2,1,0:T(8,128)(2,1)S(1)}, u32[]{:S(2)}, u32[]{:S(2)}) collective-permute-start(bf16[6,8,256]{2,1,0:T(8,128)(2,1)S(1)} %gather_fusion.4), channel_id=1, source_target_pairs={{0,16},{16,0},{32,48},{48,32},{64,80},{80,64},{96,112},{112,96},{1... | collective-permute-start | bytes 73736 | tf_op jit(solution)/shard_map/ppermute | solution.py:28
  108.4 1.5 copy-start.5
  115.7 27.0 %copy-start.3 = (bf16[8,12,256]{2,0,1:T(8,128)(2,1)}, bf16[8,12,256]{2,0,1:T(8,128)(2,1)S(1)}, u32[]{:S(2)}) copy-start(bf16[8,12,256]{2,0,1:T(8,128)(2,1)S(1)} %fusion.67) | copy-start | bytes 147460
  116.3 3.1 %collective-permute-start.3 = (bf16[6,3584]{1,0:T(8,128)(2,1)S(1)}, bf16[6,3584]{1,0:T(8,128)(2,1)S(1)}, u32[]{:S(2)}, u32[]{:S(2)}) collective-permute-start(bf16[6,3584]{1,0:T(8,128)(2,1)S(1)} %gather_fusion.6), channel_id=1, source_target_pairs={{0,16},{16,0},{32,48},{48,32},{64,80},{80,64},{96,112},{112,96},{1... | collective-permute-start | bytes 129032 | tf_op jit(solution)/shard_map/ppermute | solution.py:28
  146.9 0.7 copy-start.8

commit v2 on v1

--- a/solution.py
+++ b/solution.py
@@ -98,16 +98,53 @@
     offset = 0
     for piece in pieces:
         size = piece.size
-        part = gathered[:, offset : offset + size].reshape((groups,) + piece.shape)
-        parts.append(part)
+        part = gathered[:, offset : offset + size]
+        parts.append(part.reshape((groups * piece.shape[0],) + piece.shape[1:]))
         offset += size
     return parts
 
 
-def merge_chans(part, chan_dim):
-    moved = jnp.moveaxis(part, 0, chan_dim)
-    shape = moved.shape
-    return moved.reshape(shape[:chan_dim] + (shape[chan_dim] * shape[chan_dim + 1],) + shape[chan_dim + 2 :])
+def place_matrix(spots, width):
+    columns = lax.broadcasted_iota(jnp.int32, (spots.shape[0], width), 1)
+    return (columns == spots[:, None]).astype(jnp.bfloat16)
+
+
+def interior_spots(first, count):
+    pixel = jnp.arange(first, first + count, dtype=jnp.int32)
+    return (pixel // SIDE + 1) * (SIDE + 2) + pixel % SIDE + 1
+
+
+def rim_spots():
+    k = jnp.arange(SIDE, dtype=jnp.int32) + 1
+    row = SIDE + 2
+    return jnp.concatenate([k, k * row + SIDE + 1, (SIDE + 1) * row + k, k * row])
+
+
+def placed(pieces):
+    width = (SIDE + 2) * (SIDE + 2) + 2
+    total = None
+    for piece, spots in pieces:
+        term = jnp.einsum(
+            "cbq,qp->cbp", piece, place_matrix(spots, width), preferred_element_type=jnp.float32
+        )
+        total = term if total is None else total + term
+    return total.astype(jnp.bfloat16)
+
+
+def conv_cm(weight, padded):
+    row_width = SIDE + 2
+    out_span = SIDE * row_width
+    accum = None
+    for tap_index in range(9):
+        offset = tap_index // 3 * row_width + tap_index % 3
+        term = jnp.einsum(
+            "oc,cbp->bop",
+            weight[tap_index],
+            padded[:, :, offset : offset + out_span],
+            preferred_element_type=jnp.float32,
+        )
+        accum = term if accum is None else accum + term
+    return accum
 
 
 def local(
@@ -161,14 +198,18 @@
     turn_codes = lax.dynamic_slice_in_dim(rotations, first_tile, per_dev, 0)
     local_adjacent = (adjacent // per_dev - tile_group + 1) % groups * per_dev + adjacent % per_dev
     rim_cells = pick_rims(widened, local_adjacent, turn_codes)
+    rims_cm = jnp.transpose(rim_cells, (2, 0, 1, 3)).reshape(
+        atmos_local + ocean_local, per_dev, 4 * SIDE
+    )
 
     early = 2 * SIDE
+    pixels = SIDE * SIDE
+    ocean_cm = jnp.transpose(own_ocean, (1, 0, 2))
     atmos_int, atmos_rims, ocean_head = gather_rows(
-        [atmos_state, rim_cells[:, :, :atmos_local], own_ocean[:, :, :early]]
-    )
-    atmos_pad = pad_tile(merge_chans(atmos_int, 1), merge_chans(atmos_rims, 2))
-    atmos_start = jnp.zeros((per_dev, atmos_weight.shape[1], SIDE * (SIDE + 2)), jnp.float32)
-    atmos_accum = conv_step(atmos_weight, atmos_start, atmos_pad)
+        [jnp.transpose(atmos_state, (1, 0, 2)), rims_cm[:atmos_local], ocean_cm[:, :, :early]]
+    )
+    atmos_pad = placed([(atmos_int, interior_spots(0, pixels)), (atmos_rims, rim_spots())])
+    atmos_accum = conv_cm(atmos_weight, atmos_pad)
     atmos_next = (
         atmos_state.astype(jnp.float32) + jax.nn.gelu(trim_columns(atmos_accum), approximate=True)
     ).astype(jnp.bfloat16)
@@ -180,17 +221,23 @@
     late_own = jnp.where(
         from_here[:, None], late_block[own_tile], partner(late_block[send_tile], "tiles", 0)
     )
-    forcing = late_own[:, : late_block.shape[1] - sea_width].reshape(per_owner, atmos_local, SIDE * SIDE)
+    forcing = late_own[:, : late_block.shape[1] - sea_width].reshape(per_owner, atmos_local, pixels)
     own_rims = late_own[:, late_block.shape[1] - sea_width :].reshape(per_owner, 4, ocean_local, SIDE)
-
-    ocean_tail, ocean_rims, force_parts = gather_rows([own_ocean[:, :, early:], own_rims, forcing])
-    ocean_full = jnp.concatenate([merge_chans(ocean_head, 1), merge_chans(ocean_tail, 1)], axis=2)
-    ocean_pad = pad_tile(ocean_full, merge_chans(ocean_rims, 2))
-    force_all = merge_chans(force_parts, 1)
-    conv_start = jnp.zeros((per_owner, ocean_weight.shape[1], SIDE * (SIDE + 2)), jnp.float32)
-    conv_accum = conv_step(ocean_weight, conv_start, ocean_pad)
+    own_rims = jnp.transpose(own_rims, (2, 0, 1, 3)).reshape(ocean_local, per_owner, 4 * SIDE)
+
+    ocean_tail, ocean_rims, force_all = gather_rows(
+        [ocean_cm[:, :, early:], own_rims, jnp.transpose(forcing, (1, 0, 2))]
+    )
+    ocean_pad = placed(
+        [
+            (ocean_head, interior_spots(0, early)),
+            (ocean_tail, interior_spots(early, pixels - early)),
+            (ocean_rims, rim_spots()),
+        ]
+    )
+    conv_accum = conv_cm(ocean_weight, ocean_pad)
     couple_accum = jnp.einsum(
-        "oc,bcp->bop", couple_weight, force_all, preferred_element_type=jnp.float32
+        "oc,cbp->bop", couple_weight, force_all, preferred_element_type=jnp.float32
     )
     mixed = trim_columns(conv_accum) + couple_accum
     ocean_next = (own_ocean.astype(jnp.float32) + jax.nn.gelu(mixed, approximate=True)).astype(

time: 153 us -> 101 us (0.66)
  local copies, waits for them, and re-layouts: 62.6 us -> 23.9 us
  other arithmetic: 17.2 us -> 4.29 us
    another operation x7 -> x2, local copies, waits for them, and re-layouts: 17.6 us -> 0.2 us  [the longest x1 5.88 us: pad_tile(): tile_grid = tile_field.reshape(tile_count, chan_count, SIDE, SIDE)]
    concatenate x4 -> x1, other arithmetic: 13.2 us -> 0.08 us  [rim_spots(): jnp.concatenate([k, k * row + SIDE + 1, (SIDE + 1) * row + k, k * row])]
    concatenate x2 -> x0, local copies, waits for them, and re-layouts: 12.1 us -> none  [the longest x1 11.9 us: pad_tile(): jnp.concatenate([rim_cells[:, 3][:, :, :, None], tile_grid, rim_cells[:,...]
    reshape x13 -> x8, local copies, waits for them, and re-layouts: 10.2 us -> 2.93 us  [the longest x6 2.81 us: gather_rows(): parts.append(part.reshape((groups * piece.shape[0],) + piece.shape[1:]))]
    transpose x3 -> x0, local copies, waits for them, and re-layouts: 5.42 us -> none  [merge_chans(): moved = jnp.moveaxis(part, 0, chan_dim)]
    slice x10 -> x13, local copies, waits for them, and re-layouts: 0.31 us -> 3.33 us  [the longest x1 2.97 us: conv_cm(): padded[:, :, offset:offset + out_span]]
    unnamed x27 -> x26, local copies, waits for them, and re-layouts: 3.81 us -> 4.36 us
    dot_general x19 -> x24, matrix products: 8.22 us -> 8.19 us  [the longest x18 5.09 us: conv_cm(): jnp.einsum('oc,cbp->bop', weight[tap_index], padded[:, :, offset:offset +...]
  transfers between devices with their start and end apart: 4 -> 4, of which waited for: 1 -> 0; matrix products, arithmetic and copies ran while one was open for 8% -> 14% of each run, Pallas kernels for 0% -> 0%
where the time goes in v2:
time: 101 us; the launch traced here: 100 us
  blocking collectives  48.4 us (48%)
  local copies, waits for them, and re-layouts  23.9 us (24%)
  starting transfers between devices  12.8 us (13%)
  matrix products  8.19 us (8%)
  other arithmetic  4.29 us (4%)
  between operations  2.62 us (3%)
    all_gather x2, blocking collectives, gather_rows(): gathered = lax.all_gather(rows, 'chan', axis=0, tiled=False)  48.4 us
    ppermute x1, starting transfers between devices, padded_2(): lax.ppermute(head, axis, [((i + 1) % count, i) for i in range(count)])  8.95 us
    dot_general x18, matrix products, conv_cm(): jnp.einsum('oc,cbp->bop', weight[tap_index], padded[:, :, offset:offset +...  5.09 us
    unnamed x26, local copies, waits for them, and re-layouts  4.36 us
    ppermute x2, starting transfers between devices, partner(): return lax.ppermute(value, axis, pairs)  3.84 us
    slice x1, local copies, waits for them, and re-layouts, conv_cm(): padded[:, :, offset:offset + out_span]  2.97 us
    reshape x6, local copies, waits for them, and re-layouts, gather_rows(): parts.append(part.reshape((groups * piece.shape[0],) + piece.shape[1:]))  2.81 us
    dot_general x5, matrix products, placed(): jnp.einsum('cbq,qp->cbp', piece, place_matrix(spots, width), preferred_el...  2.27 us
  transfers between devices with their start and end apart: 4, of which 0 were waited for; matrix products, arithmetic and copies ran while one was open for 14% of the time, Pallas kernels for 0%

profile of v2, /device:TPU:6, one launch (start us, length us, event | category | flops | bytes accessed | tf_op | source)
XLA Modules:
  0.0 100.2 jit_solution(15670977796543498152)
XLA Ops:
  0.7 0.8 dynamic-slice_convert_fusion
  1.4 0.8 broadcast_multiply_fusion
  2.7 1.1 %copy.118 = bf16[8,12,256]{1,2,0:T(8,128)(2,1)S(1)} copy(bf16[8,12,256]{2,0,1:T(8,128)(2,1)} %param.8) | data formatting | bytes 98304 | tf_op args[0]
  5.5 8.9 %collective-permute-start.1 = (bf16[8,1280]{1,0:T(8,128)(2,1)S(1)}, bf16[8,1280]{1,0:T(8,128)(2,1)S(1)}, u32[]{:S(2)}, u32[]{:S(2)}) collective-permute-start(bf16[8,1280]{1,0:T(8,128)(2,1)S(1)} %reshape.317), channel_id=1, source_target_pairs={{16,0},{32,16},{48,32},{64,48},{80,64},{96,80},{112,96},{128,112},... | collective-permute-start | bytes 61448 | tf_op jit(solution)/shard_map/ppermute | solution.py:18
  15.1 1.4 %scatter_custom_fusion = s32[192]{0:T(256)S(1)} fusion(s32[256]{0:T(256)S(1)} %compare_select_fusion.1, s32[256]{0:T(256)S(1)} %iota.62, s32[]{:T(128)} %constant.178.clone.1), kind=kCustom, calls=%fused_computation.220 | custom fusion | bytes 772 | tf_op jit(solution)/shard_map/scatter | solution.py:175
  16.5 0.6 gather_fusion.3
  17.8 1.9 %collective-permute-start.2 = (bf16[6,8,256]{2,1,0:T(8,128)(2,1)S(1)}, bf16[6,8,256]{2,1,0:T(8,128)(2,1)S(1)}, u32[]{:S(2)}, u32[]{:S(2)}) collective-permute-start(bf16[6,8,256]{2,1,0:T(8,128)(2,1)S(1)} %gather_fusion.4), channel_id=1, source_target_pairs={{0,16},{16,0},{32,48},{48,32},{64,80},{80,64},{96,112},{112,96},{1... | collective-permute-start | bytes 73736 | tf_op jit(solution)/shard_map/ppermute | solution.py:28
  20.3 0.6 gather_fusion.1
  21.0 0.6 dynamic_slice.19
  21.9 0.6 dynamic_slice.18
  23.8 0.7 compare_and_fusion
  26.6 0.6 gather_fusion
  29.4 0.7 rev.3
  30.9 24.9 %all_gather.6 = bf16[16,126,256]{2,1,0:T(8,128)(2,1)S(1)} all-gather(bf16[1,126,256]{2,1,0:T(8,128)(2,1)S(1)} %all_gather_reshape.6), channel_id=1, replica_groups=mesh['tiles'=32,'chan'=16] {'chan'}, dimensions={0}, use_global_device_ids=true | all-gather | bytes 1096704 | tf_op jit(solution)/shard_map/all_gather | solution.py:94
  55.8 0.6 copy.163
  57.4 0.6 fusion.61
  58.6 3.0 %fusion.163 = (bf16[192,8,288]{2,1,0:T(8,128)(2,1)S(1)}, bf16[192,8,288]{2,1,0:T(8,128)(2,1)S(1)}, bf16[192,8,288]{2,1,0:T(8,128)(2,1)S(1)}, bf16[192,8,288]{2,1...) fusion(bf16[192,8,326]{2,1,0:T(8,128)(2,1)S(1)} %add_convert_fusion), kind=kLoop, calls=%fused_computation.226 | loop fusion | bytes 15925248 | tf_op jit(solution)/shard_map/slice | solution.py:143
  65.0 0.6 gather_fusion.6
  65.6 1.9 %collective-permute-start.3 = (bf16[6,3584]{1,0:T(8,128)(2,1)S(1)}, bf16[6,3584]{1,0:T(8,128)(2,1)S(1)}, u32[]{:S(2)}, u32[]{:S(2)}) collective-permute-start(bf16[6,3584]{1,0:T(8,128)(2,1)S(1)} %gather_fusion.6), channel_id=1, source_target_pairs={{0,16},{16,0},{32,48},{48,32},{64,80},{80,64},{96,112},{112,96},{1... | collective-permute-start | bytes 129032 | tf_op jit(solution)/shard_map/ppermute | solution.py:28
  68.0 0.6 gather_fusion.5
  69.1 23.5 %all_gather.7 = bf16[16,126,256]{2,1,0:T(8,128)(2,1)S(1)} all-gather(bf16[1,126,256]{2,1,0:T(8,128)(2,1)S(1)} %all_gather_reshape.7), channel_id=1, replica_groups=mesh['tiles'=32,'chan'=16] {'chan'}, dimensions={0}, use_global_device_ids=true | all-gather | bytes 1096704 | tf_op jit(solution)/shard_map/all_gather | solution.py:94
  93.5 0.8 reshape.338
  98.0 0.9 reshape.342
  99.4 0.8 add_convert_fusion.1
  (152 shorter events, 20.0 us)
Async XLA Ops:
  0.6 98.8 %copy-start = (bf16[8,192]{1,0:T(8,128)(2,1)S(1)}, bf16[8,192]{1,0:T(8,128)(2,1)}, u32[]{:S(2)}) copy-start(bf16[8,192]{1,0:T(8,128)(2,1)} %param.12) | copy-start | bytes 9220
  2.7 11.8 %copy-start.4 = (s32[256]{0:T(256)S(1)}, s32[256]{0:T(256)}, u32[]{:S(2)}) copy-start(s32[256]{0:T(256)} %param.13) | copy-start | bytes 3076
  3.8 13.4 %copy-start.2 = (bf16[8,8,256]{2,1,0:T(8,128)(2,1)S(1)}, bf16[8,8,256]{2,1,0:T(8,128)(2,1)}, u32[]{:S(2)}) copy-start(bf16[8,8,256]{2,1,0:T(8,128)(2,1)} %param.9) | copy-start | bytes 98308
  3.8 16.0 %copy-start.5 = (s32[256,4]{0,1:T(4,128)S(1)}, s32[256,4]{0,1:T(4,128)}, u32[]{:S(2)}) copy-start(s32[256,4]{0,1:T(4,128)} %param.14) | copy-start | bytes 12292
  3.9 16.3 %copy-start.6 = (s32[256,4]{0,1:T(4,128)S(1)}, s32[256,4]{0,1:T(4,128)}, u32[]{:S(2)}) copy-start(s32[256,4]{0,1:T(4,128)} %param.15) | copy-start | bytes 12292
  4.8 20.7 %copy-start.1 = (bf16[8,12,256]{2,0,1:T(8,128)(2,1)S(1)}, bf16[8,12,256]{2,0,1:T(8,128)(2,1)}, u32[]{:S(2)}) copy-start(bf16[8,12,256]{2,0,1:T(8,128)(2,1)} %param.8) | copy-start | bytes 147460
  5.5 20.5 %collective-permute-start.1 = (bf16[8,1280]{1,0:T(8,128)(2,1)S(1)}, bf16[8,1280]{1,0:T(8,128)(2,1)S(1)}, u32[]{:S(2)}, u32[]{:S(2)}) collective-permute-start(bf16[8,1280]{1,0:T(8,128)(2,1)S(1)} %reshape.317), channel_id=1, source_target_pairs={{16,0},{32,16},{48,32},{64,48},{80,64},{96,80},{112,96},{128,112},... | collective-permute-start | bytes 61448 | tf_op jit(solution)/shard_map/ppermute | solution.py:18
  14.5 11.0 %collective-permute-start = (bf16[8,1280]{1,0:T(8,128)(2,1)S(1)}, bf16[8,1280]{1,0:T(8,128)(2,1)S(1)}, u32[]{:S(2)}, u32[]{:S(2)}) collective-permute-start(bf16[8,1280]{1,0:T(8,128)(2,1)S(1)} %reshape.317), channel_id=1, source_target_pairs={{0,16},{16,32},{32,48},{48,64},{64,80},{80,96},{96,112},{112,128},... | collective-permute-start | bytes 61448 | tf_op jit(solution)/shard_map/ppermute | solution.py:16
  17.8 12.9 %collective-permute-start.2 = (bf16[6,8,256]{2,1,0:T(8,128)(2,1)S(1)}, bf16[6,8,256]{2,1,0:T(8,128)(2,1)S(1)}, u32[]{:S(2)}, u32[]{:S(2)}) collective-permute-start(bf16[6,8,256]{2,1,0:T(8,128)(2,1)S(1)} %gather_fusion.4), channel_id=1, source_target_pairs={{0,16},{16,0},{32,48},{48,32},{64,80},{80,64},{96,112},{112,96},{1... | collective-permute-start | bytes 73736 | tf_op jit(solution)/shard_map/ppermute | solution.py:28
  58.6 3.0 %copy-start.7 = (bf16[9,12,192]{2,1,0:T(8,128)(2,1)S(1)}, bf16[9,12,192]{2,1,0:T(8,128)(2,1)}, u32[]{:S(2)}) copy-start(bf16[9,12,192]{2,1,0:T(8,128)(2,1)} %param.10) | copy-start | bytes 124420
  65.0 3.6 %copy-start.3 = (bf16[8,12,256]{2,0,1:T(8,128)(2,1)}, bf16[8,12,256]{2,0,1:T(8,128)(2,1)S(1)}, u32[]{:S(2)}) copy-start(bf16[8,12,256]{2,0,1:T(8,128)(2,1)S(1)} %fusion.80) | copy-start | bytes 147460
  65.6 3.1 %collective-permute-start.3 = (bf16[6,3584]{1,0:T(8,128)(2,1)S(1)}, bf16[6,3584]{1,0:T(8,128)(2,1)S(1)}, u32[]{:S(2)}, u32[]{:S(2)}) collective-permute-start(bf16[6,3584]{1,0:T(8,128)(2,1)S(1)} %gather_fusion.6), channel_id=1, source_target_pairs={{0,16},{16,0},{32,48},{48,32},{64,80},{80,64},{96,112},{112,96},{1... | collective-permute-start | bytes 129032 | tf_op jit(solution)/shard_map/ppermute | solution.py:28
  94.7 0.7 copy-start.8

commit v3 on v2

--- a/solution.py
+++ b/solution.py
@@ -134,17 +134,19 @@
 def conv_cm(weight, padded):
     row_width = SIDE + 2
     out_span = SIDE * row_width
+    taps, out_chans, in_chans = weight.shape
+    products = jnp.einsum(
+        "kc,cbp->kbp",
+        weight.reshape(taps * out_chans, in_chans),
+        padded,
+        preferred_element_type=jnp.float32,
+    ).reshape(taps, out_chans, padded.shape[1], padded.shape[2])
     accum = None
-    for tap_index in range(9):
+    for tap_index in range(taps):
         offset = tap_index // 3 * row_width + tap_index % 3
-        term = jnp.einsum(
-            "oc,cbp->bop",
-            weight[tap_index],
-            padded[:, :, offset : offset + out_span],
-            preferred_element_type=jnp.float32,
-        )
+        term = products[tap_index, :, :, offset : offset + out_span]
         accum = term if accum is None else accum + term
-    return accum
+    return jnp.transpose(accum, (1, 0, 2))
 
 
 def local(
@@ -165,34 +167,35 @@
     first_tile = tile_group * per_dev
     per_owner = per_dev * 3 // 4
     ocean_total = per_owner * groups
-    counts = jnp.sum(sea_mask.reshape(groups, per_dev), axis=1)
-    starts = jnp.cumsum(counts) - counts
-    sea_rank = jnp.cumsum(sea_mask) - 1
-    rank_spots = jnp.where(sea_mask == 1, sea_rank, ocean_total)
-    tile_of_rank = (
-        jnp.zeros((ocean_total,), jnp.int32)
-        .at[rank_spots]
-        .set(jnp.arange(sea_mask.shape[0], dtype=jnp.int32), mode="drop")
-    )
-    my_first = starts[tile_group]
-    my_last = my_first + counts[tile_group]
+    sea_count = jnp.cumsum(sea_mask)
     parity = tile_group % 2
     pair_base = tile_group // 2 * 2 * per_owner
     slot_ids = jnp.arange(per_owner, dtype=jnp.int32)
-    ranks_send = pair_base + 2 * slot_ids + (1 - parity)
-    ranks_own = pair_base + 2 * slot_ids + parity
-    send_tile = jnp.clip(tile_of_rank[ranks_send] - first_tile, 0, per_dev - 1)
-    own_tile = jnp.clip(tile_of_rank[ranks_own] - first_tile, 0, per_dev - 1)
-    from_here = (ranks_own >= my_first) & (ranks_own < my_last)
-
-    own_ocean = jnp.where(
-        from_here[:, None, None], ocean_state[own_tile], partner(ocean_state[send_tile], "tiles", 0)
-    )
+    ranks = jnp.concatenate(
+        [pair_base + 2 * slot_ids + (1 - parity), pair_base + 2 * slot_ids + parity]
+    )
+    tiles_of = jnp.sum((sea_count[None, :] <= ranks[:, None]).astype(jnp.int32), axis=1)
+    send_tile = jnp.clip(tiles_of[:per_owner] - first_tile, 0, per_dev - 1)
+    own_tile = jnp.clip(tiles_of[per_owner:] - first_tile, 0, per_dev - 1)
+    from_here = tiles_of[per_owner:] // per_dev == tile_group
 
     sea_here = lax.dynamic_slice_in_dim(sea_mask, first_tile, per_dev, 0)
     sea_field = ocean_state * sea_here.astype(jnp.bfloat16)[:, None, None]
     edge_strips = jnp.concatenate([edge_set(atmos_state), edge_set(sea_field)], axis=1)
-    widened = padded_2(edge_strips.reshape(per_dev, -1), (("tiles", 0),), per_dev)
+    edge_flat = edge_strips.reshape(-1)
+    outgoing = jnp.concatenate([edge_flat, ocean_state[send_tile].reshape(-1)])
+    from_left = lax.ppermute(outgoing, "tiles", [(i, (i + 1) % groups) for i in range(groups)])
+    from_right = lax.ppermute(outgoing, "tiles", [((i + 1) % groups, i) for i in range(groups)])
+    edge_size = edge_flat.shape[0]
+    partner_ocean = jnp.where(parity == 0, from_right[edge_size:], from_left[edge_size:])
+    own_ocean = jnp.where(
+        from_here[:, None, None],
+        ocean_state[own_tile],
+        partner_ocean.reshape((per_owner,) + ocean_state.shape[1:]),
+    )
+    widened = jnp.concatenate(
+        [from_left[:edge_size], edge_flat, from_right[:edge_size]]
+    )
     widened = widened.reshape(3 * per_dev, atmos_local + ocean_local, 4, SIDE)
     adjacent = lax.dynamic_slice_in_dim(neighbours, first_tile, per_dev, 0)
     turn_codes = lax.dynamic_slice_in_dim(rotations, first_tile, per_dev, 0)

time: 101 us -> 96.1 us (0.951)
  local copies, waits for them, and re-layouts: 23.9 us -> 20 us
  other arithmetic: 4.29 us -> 6.68 us
  starting transfers between devices: 12.8 us -> 10.9 us
  matrix products: 8.19 us -> 6.76 us
  waiting for transfers between devices: 0.01 us -> 1.39 us
  between operations: 2.62 us -> 1.41 us
    slice x2 -> x3, local copies, waits for them, and re-layouts: 3.04 us -> 0.08 us  [the longest x1 2.97 us: conv_cm(): padded[:, :, offset:offset + out_span]]
    dot_general x0 -> x1, local copies, waits for them, and re-layouts: none -> 1.96 us  [conv_cm(): jnp.einsum('kc,cbp->kbp', weight.reshape(taps * out_chans, in_chans), pad...]
    ppermute x2 -> x1, starting transfers between devices: 3.84 us -> 1.92 us  [partner(): return lax.ppermute(value, axis, pairs)]
    add x3, other arithmetic: 0.02 us -> 1.67 us  [interior_spots(): return (pixel // SIDE + 1) * (SIDE + 2) + pixel % SIDE + 1]
    scatter x1 -> x0, local copies, waits for them, and re-layouts: 1.4 us -> none  [local(): tile_of_rank = jnp.zeros((ocean_total,), jnp.int32).at[rank_spots].set(jn...]
    ppermute x2, waiting for transfers between devices: 0.01 us -> 1.38 us  [the longest x1 1.38 us: local(): lax.ppermute(outgoing, 'tiles', [(i, (i + 1) % groups) for i in range(gro...]
    dot_general x18 -> x2, matrix products: 5.09 us -> 3.9 us  [conv_cm(): jnp.einsum('kc,cbp->kbp', weight.reshape(taps * out_chans, in_chans), pad...]
    dynamic_slice x2 -> x0, local copies, waits for them, and re-layouts: 1.18 us -> none  [the longest x1 0.59 us: local(): my_last = my_first + counts[tile_group]]
  transfers between devices with their start and end apart: 4 -> 3, of which waited for: 0 -> 1; matrix products, arithmetic and copies ran while one was open for 14% -> 5% of each run, Pallas kernels for 0% -> 0%
where the time goes in v3:
time: 96.1 us; the launch traced here: 95.1 us
  blocking collectives  48 us (50%)
  local copies, waits for them, and re-layouts  20 us (21%)
  starting transfers between devices  10.9 us (11%)
  matrix products  6.76 us (7%)
  other arithmetic  6.68 us (7%)
  between operations  1.41 us (1%)
  waiting for transfers between devices  1.39 us (1%)
    all_gather x2, blocking collectives, gather_rows(): gathered = lax.all_gather(rows, 'chan', axis=0, tiled=False)  48 us
    ppermute x1, starting transfers between devices, local(): lax.ppermute(outgoing, 'tiles', [((i + 1) % groups, i) for i in range(gro...  8.95 us
    unnamed x46, local copies, waits for them, and re-layouts  4.09 us
    dot_general x2, matrix products, conv_cm(): jnp.einsum('kc,cbp->kbp', weight.reshape(taps * out_chans, in_chans), pad...  3.9 us
    reshape x6, local copies, waits for them, and re-layouts, gather_rows(): parts.append(part.reshape((groups * piece.shape[0],) + piece.shape[1:]))  3.57 us
    dot_general x3, matrix products, placed(): jnp.einsum('cbq,qp->cbp', piece, place_matrix(spots, width), preferred_el...  2.04 us
    dot_general x1, local copies, waits for them, and re-layouts, conv_cm(): jnp.einsum('kc,cbp->kbp', weight.reshape(taps * out_chans, in_chans), pad...  1.96 us
  transfers between devices with their start and end apart: 3, of which 1 were waited for; matrix products, arithmetic and copies ran while one was open for 5% of the time, Pallas kernels for 0%

profile of v3, /device:TPU:6, one launch (start us, length us, event | category | flops | bytes accessed | tf_op | source)
XLA Modules:
  0.0 95.1 jit_solution(13495925430718279353)
XLA Ops:
  0.7 0.8 dynamic-slice_convert_fusion
  1.5 0.8 broadcast_multiply_fusion
  2.7 1.1 %copy.159 = bf16[8,12,256]{1,2,0:T(8,128)(2,1)S(1)} copy(bf16[8,12,256]{2,0,1:T(8,128)(2,1)} %param.8) | data formatting | bytes 98304 | tf_op args[0]
  4.0 1.0 %reduce-window.9 = s32[2,128]{1,0:T(2,128)S(1)} reduce-window(s32[2,128]{1,0:T(2,128)} %bitcast.130, s32[]{:T(128)} %constant.178.clone.1), window={size=1x128 pad=0_0x127_0}, to_apply=%region_0.0 | reduce-window | flops 32512 | bytes 2052 | tf_op jit(solution)/shard_map/reduce-window
  5.6 1.3 %gather_fusion = bf16[6,8,256]{2,1,0:T(8,128)(2,1)S(1)} fusion(bf16[8,8,256]{2,1,0:T(8,128)(2,1)} %param.9, s32[1024]{0:T(1024)S(1)} %pad_clamp_fusion.2), kind=kCustom, calls=%fused_computation | custom fusion | bytes 49176 | tf_op jit(solution)/shard_map/gather | solution.py:186
  8.5 8.9 %collective-permute-start.1 = (bf16[22528]{0:T(1024)(128)(2,1)S(1)}, bf16[22528]{0:T(1024)(128)(2,1)S(1)}, u32[]{:S(2)}, u32[]{:S(2)}) collective-permute-start(bf16[22528]{0:T(1024)(128)(2,1)S(1)} %constant_dynamic-update-slice_fusion), channel_id=1, source_target_pairs={{16,0},{32,16},{48,32},{64,48},{80,64},{96,80},{112,96},{128,112},... | collective-permute-start | bytes 135176 | tf_op jit(solution)/shard_map/ppermute | solution.py:188
  20.8 1.4 %collective-permute-done = bf16[22528]{0:T(1024)(128)(2,1)S(1)} collective-permute-done((bf16[22528]{0:T(1024)(128)(2,1)S(1)}, bf16[22528]{0:T(1024)(128)(2,1)S(1)}, u32[]{:S(2)}, u32[]{:S(2)}) %collective-permute-start) | collective-permute-done | bytes 45088 | tf_op jit(solution)/shard_map/ppermute | solution.py:187
  23.5 0.6 gather_fusion.1
  26.2 0.7 rev.3
  27.4 24.7 %all_gather.6 = bf16[16,126,256]{2,1,0:T(8,128)(2,1)S(1)} all-gather(bf16[1,126,256]{2,1,0:T(8,128)(2,1)S(1)} %all_gather_reshape.6), channel_id=1, replica_groups=mesh['tiles'=32,'chan'=16] {'chan'}, dimensions={0}, use_global_device_ids=true | all-gather | bytes 1096704 | tf_op jit(solution)/shard_map/all_gather | solution.py:94
  52.2 0.6 copy.200
  53.4 1.1 %reshape.252 = bf16[192,8,64]{2,1,0:T(8,128)(2,1)} reshape(bf16[16,6144]{1,0:T(8,128)(2,1)S(1)} %slice.256) | data formatting | bytes 393216 | tf_op jit(solution)/shard_map/reshape | solution.py:102
  54.7 1.3 %fusion.2 = f32[192,8,326]{2,0,1:T(8,128)S(1)} fusion(bf16[192,8,256]{2,1,0:T(8,128)(2,1)S(1)} %reshape.251, s32[256]{0:T(256)} %fusion.67), kind=kOutput, calls=%fused_computation.13 | convolution fusion | flops 256460288 | bytes 2790400 | tf_op jit(solution)/shard_map/cbq,qp->cbp/dot_general | solution.py:127
  56.0 3.2 %convolution_bitcast_fusion = f32[108,8,326]{0,2,1:T(8,128)} fusion(f32[192,8,326]{2,0,1:T(8,128)S(1)} %fusion.2, bf16[192,8,64]{2,1,0:T(8,128)(2,1)} %reshape.252, bf16[108,192]{1,0:T(8,128)(2,1)S(1)} %reshape.253, s32[64]{0:T(128)S(1)} %pad_add_fusion.1), kind=kOutput, calls=%fused_computation.6 | convolution fusion | flops 173275520 | bytes 3367936 | tf_op jit(solution)/shard_map/kc,cbp->kbp/dot_general | solution.py:138
  59.1 2.0 %copy.183 = f32[108,8,326]{2,1,0:T(8,128)S(1)} copy(f32[108,8,326]{0,2,1:T(8,128)} %convolution_bitcast_fusion) | data formatting | bytes 2253312 | tf_op jit(solution)/shard_map/kc,cbp->kbp/dot_general | solution.py:138
  62.4 0.6 gather_fusion.4
  63.0 1.9 %collective-permute-start.2 = (bf16[6,3584]{1,0:T(8,128)(2,1)S(1)}, bf16[6,3584]{1,0:T(8,128)(2,1)S(1)}, u32[]{:S(2)}, u32[]{:S(2)}) collective-permute-start(bf16[6,3584]{1,0:T(8,128)(2,1)S(1)} %gather_fusion.4), channel_id=1, source_target_pairs={{0,16},{16,0},{32,48},{48,32},{64,80},{80,64},{96,112},{112,96},{1... | collective-permute-start | bytes 129032 | tf_op jit(solution)/shard_map/ppermute | solution.py:28
  65.4 0.6 gather_fusion.3
  66.6 23.2 %all_gather.7 = bf16[16,126,256]{2,1,0:T(8,128)(2,1)S(1)} all-gather(bf16[1,126,256]{2,1,0:T(8,128)(2,1)S(1)} %all_gather_reshape.7), channel_id=1, replica_groups=mesh['tiles'=32,'chan'=16] {'chan'}, dimensions={0}, use_global_device_ids=true | all-gather | bytes 1096704 | tf_op jit(solution)/shard_map/all_gather | solution.py:94
  89.8 0.6 copy.201
  90.7 0.8 reshape.265
  91.9 0.7 convolution_bitcast_fusion.1
  92.9 0.9 reshape.271
  94.2 0.8 add_convert_fusion.1
  (146 shorter events, 14.0 us)
Async XLA Ops:
  0.6 91.2 %copy-start = (bf16[9,8,128]{2,1,0:T(8,128)(2,1)S(1)}, bf16[9,8,128]{2,1,0:T(8,128)(2,1)}, u32[]{:S(2)}) copy-start(bf16[9,8,128]{2,1,0:T(8,128)(2,1)} %param.11) | copy-start | bytes 55300
  0.6 19.5 %copy-start.2 = (bf16[8,8,256]{2,1,0:T(8,128)(2,1)S(1)}, bf16[8,8,256]{2,1,0:T(8,128)(2,1)}, u32[]{:S(2)}) copy-start(bf16[8,8,256]{2,1,0:T(8,128)(2,1)} %param.9) | copy-start | bytes 98308
  0.7 20.0 %copy-start.1 = (bf16[8,12,256]{2,0,1:T(8,128)(2,1)S(1)}, bf16[8,12,256]{2,0,1:T(8,128)(2,1)}, u32[]{:S(2)}) copy-start(bf16[8,12,256]{2,0,1:T(8,128)(2,1)} %param.8) | copy-start | bytes 147460
  0.7 18.6 %copy-start.14 = (s32[256,4]{0,1:T(4,128)S(1)}, s32[256,4]{0,1:T(4,128)}, u32[]{:S(2)}) copy-start(s32[256,4]{0,1:T(4,128)} %param.14) | copy-start | bytes 12292
  0.7 18.9 %copy-start.15 = (s32[256,4]{0,1:T(4,128)S(1)}, s32[256,4]{0,1:T(4,128)}, u32[]{:S(2)}) copy-start(s32[256,4]{0,1:T(4,128)} %param.15) | copy-start | bytes 12292
  0.7 20.1 %copy-start.10 = (bf16[9,12,192]{2,1,0:T(8,128)(2,1)S(1)}, bf16[9,12,192]{2,1,0:T(8,128)(2,1)}, u32[]{:S(2)}) copy-start(bf16[9,12,192]{2,1,0:T(8,128)(2,1)} %param.10) | copy-start | bytes 124420
  8.5 12.2 %collective-permute-start.1 = (bf16[22528]{0:T(1024)(128)(2,1)S(1)}, bf16[22528]{0:T(1024)(128)(2,1)S(1)}, u32[]{:S(2)}, u32[]{:S(2)}) collective-permute-start(bf16[22528]{0:T(1024)(128)(2,1)S(1)} %constant_dynamic-update-slice_fusion), channel_id=1, source_target_pairs={{16,0},{32,16},{48,32},{64,48},{80,64},{96,80},{112,96},{128,112},... | collective-permute-start | bytes 135176 | tf_op jit(solution)/shard_map/ppermute | solution.py:188
  17.5 4.7 %collective-permute-start = (bf16[22528]{0:T(1024)(128)(2,1)S(1)}, bf16[22528]{0:T(1024)(128)(2,1)S(1)}, u32[]{:S(2)}, u32[]{:S(2)}) collective-permute-start(bf16[22528]{0:T(1024)(128)(2,1)S(1)} %constant_dynamic-update-slice_fusion), channel_id=1, source_target_pairs={{0,16},{16,32},{32,48},{48,64},{64,80},{80,96},{96,112},{112,128},... | collective-permute-start | bytes 135176 | tf_op jit(solution)/shard_map/ppermute | solution.py:187
  18.2 6.1 %copy-start.11 = (pred[6]{0:T(512)(128)(4,1)}, pred[6]{0:T(512)(128)(4,1)S(1)}, u32[]{:S(2)}) copy-start(pred[6]{0:T(512)(128)(4,1)S(1)} %fusion.76) | copy-start | bytes 22
  20.7 3.5 %copy-start.6 = (bf16[6,8,256]{2,1,0:T(8,128)(2,1)}, bf16[6,8,256]{2,1,0:T(8,128)(2,1)S(1)}, u32[]{:S(2)}) copy-start(bf16[6,8,256]{2,1,0:T(8,128)(2,1)S(1)} %gather_fusion.2) | copy-start | bytes 73732
  22.2 1.9 %copy-start.8 = (bf16[6,8,256]{2,1,0:T(8,128)(2,1)}, bf16[6,8,256]{2,1,0:T(8,128)(2,1)S(1)}, u32[]{:S(2)}) copy-start(bf16[6,8,256]{2,1,0:T(8,128)(2,1)S(1)} %select_n.158) | copy-start | bytes 73732
  22.3 1.9 %copy-start.4 = (bf16[8,6,256]{2,0,1:T(8,128)(2,1)}, bf16[8,6,256]{2,0,1:T(8,128)(2,1)S(1)}, u32[]{:S(2)}) copy-start(bf16[8,6,256]{2,0,1:T(8,128)(2,1)S(1)} %fusion.79) | copy-start | bytes 73732
  61.1 3.8 %copy-start.16 = (s32[32]{0:T(128)S(1)}, s32[32]{0:T(128)}, u32[]{:S(2)}) copy-start(s32[32]{0:T(128)} %fusion.73) | copy-start | bytes 388
  61.1 4.2 %copy-start.5 = (bf16[8,6,256]{2,0,1:T(8,128)(2,1)S(1)}, bf16[8,6,256]{2,0,1:T(8,128)(2,1)}, u32[]{:S(2)}) copy-start(bf16[8,6,256]{2,0,1:T(8,128)(2,1)} %copy-done.4) | copy-start | bytes 73732
  61.5 4.7 %copy-start.12 = (pred[6]{0:T(512)(128)(4,1)S(1)}, pred[6]{0:T(512)(128)(4,1)}, u32[]{:S(2)}) copy-start(pred[6]{0:T(512)(128)(4,1)} %copy-done.11) | copy-start | bytes 22
  62.4 28.0 %copy-start.3 = (bf16[8,12,256]{2,0,1:T(8,128)(2,1)}, bf16[8,12,256]{2,0,1:T(8,128)(2,1)S(1)}, u32[]{:S(2)}) copy-start(bf16[8,12,256]{2,0,1:T(8,128)(2,1)S(1)} %fusion.29) | copy-start | bytes 147460
  63.0 3.2 %collective-permute-start.2 = (bf16[6,3584]{1,0:T(8,128)(2,1)S(1)}, bf16[6,3584]{1,0:T(8,128)(2,1)S(1)}, u32[]{:S(2)}, u32[]{:S(2)}) collective-permute-start(bf16[6,3584]{1,0:T(8,128)(2,1)S(1)} %gather_fusion.4), channel_id=1, source_target_pairs={{0,16},{16,0},{32,48},{48,32},{64,80},{80,64},{96,112},{112,96},{1... | collective-permute-start | bytes 129032 | tf_op jit(solution)/shard_map/ppermute | solution.py:28
  89.8 1.7 %copy-start.13 = (s32[224]{0:T(256)S(1)}, s32[224]{0:T(256)}, u32[]{:S(2)}) copy-start(s32[224]{0:T(256)} %fusion.71) | copy-start | bytes 2692
  91.9 2.4 %copy-start.7 = (bf16[6,8,256]{2,1,0:T(8,128)(2,1)S(1)}, bf16[6,8,256]{2,1,0:T(8,128)(2,1)}, u32[]{:S(2)}) copy-start(bf16[6,8,256]{2,1,0:T(8,128)(2,1)} %copy-done.6) | copy-start | bytes 73732
  91.9 2.4 %copy-start.9 = (bf16[6,8,256]{2,1,0:T(8,128)(2,1)S(1)}, bf16[6,8,256]{2,1,0:T(8,128)(2,1)}, u32[]{:S(2)}) copy-start(bf16[6,8,256]{2,1,0:T(8,128)(2,1)} %copy-done.8) | copy-start | bytes 73732
  91.9 2.4 %copy-start.17 = (bf16[8,192]{1,0:T(8,128)(2,1)S(1)}, bf16[8,192]{1,0:T(8,128)(2,1)}, u32[]{:S(2)}) copy-start(bf16[8,192]{1,0:T(8,128)(2,1)} %param.12) | copy-start | bytes 9220

commit v4 on v3

--- a/solution.py
+++ b/solution.py
@@ -125,7 +125,7 @@
     total = None
     for piece, spots in pieces:
         term = jnp.einsum(
-            "cbq,qp->cbp", piece, place_matrix(spots, width), preferred_element_type=jnp.float32
+            "cbq,qp->bcp", piece, place_matrix(spots, width), preferred_element_type=jnp.float32
         )
         total = term if total is None else total + term
     return total.astype(jnp.bfloat16)
@@ -135,18 +135,38 @@
     row_width = SIDE + 2
     out_span = SIDE * row_width
     taps, out_chans, in_chans = weight.shape
+    tile_count = padded.shape[0]
     products = jnp.einsum(
-        "kc,cbp->kbp",
+        "kc,bcp->bkp",
         weight.reshape(taps * out_chans, in_chans),
         padded,
         preferred_element_type=jnp.float32,
-    ).reshape(taps, out_chans, padded.shape[1], padded.shape[2])
+    ).reshape(tile_count, taps, out_chans, padded.shape[2])
     accum = None
     for tap_index in range(taps):
         offset = tap_index // 3 * row_width + tap_index % 3
-        term = products[tap_index, :, :, offset : offset + out_span]
+        term = products[:, tap_index, :, offset : offset + out_span]
         accum = term if accum is None else accum + term
-    return jnp.transpose(accum, (1, 0, 2))
+    return accum
+
+
+def pick(selector, values, spec):
+    return jnp.einsum(spec, selector, values, preferred_element_type=jnp.float32).astype(
+        jnp.bfloat16
+    )
+
+
+def edge_matrix():
+    k = jnp.arange(SIDE, dtype=jnp.int32)
+    spots = jnp.concatenate([k, k * SIDE + SIDE - 1, (SIDE - 1) * SIDE + k, k * SIDE])
+    rows = lax.broadcasted_iota(jnp.int32, (SIDE * SIDE, 4 * SIDE), 0)
+    return (rows == spots[None, :]).astype(jnp.bfloat16)
+
+
+def pair_order(own, other, parity):
+    even = jnp.where(parity == 0, own, other)
+    odd = jnp.where(parity == 0, other, own)
+    return jnp.concatenate([even, odd], axis=0)
 
 
 def local(
@@ -162,52 +182,69 @@
     per_dev = atmos_state.shape[0]
     atmos_local = atmos_state.shape[1]
     ocean_local = ocean_state.shape[1]
+    chans = atmos_local + ocean_local
+    pixels = SIDE * SIDE
     groups = lax.axis_size("tiles")
     tile_group = lax.axis_index("tiles")
     first_tile = tile_group * per_dev
     per_owner = per_dev * 3 // 4
-    ocean_total = per_owner * groups
-    sea_count = jnp.cumsum(sea_mask)
     parity = tile_group % 2
-    pair_base = tile_group // 2 * 2 * per_owner
-    slot_ids = jnp.arange(per_owner, dtype=jnp.int32)
-    ranks = jnp.concatenate(
-        [pair_base + 2 * slot_ids + (1 - parity), pair_base + 2 * slot_ids + parity]
-    )
-    tiles_of = jnp.sum((sea_count[None, :] <= ranks[:, None]).astype(jnp.int32), axis=1)
-    send_tile = jnp.clip(tiles_of[:per_owner] - first_tile, 0, per_dev - 1)
-    own_tile = jnp.clip(tiles_of[per_owner:] - first_tile, 0, per_dev - 1)
-    from_here = tiles_of[per_owner:] // per_dev == tile_group
-
-    sea_here = lax.dynamic_slice_in_dim(sea_mask, first_tile, per_dev, 0)
-    sea_field = ocean_state * sea_here.astype(jnp.bfloat16)[:, None, None]
-    edge_strips = jnp.concatenate([edge_set(atmos_state), edge_set(sea_field)], axis=1)
-    edge_flat = edge_strips.reshape(-1)
-    outgoing = jnp.concatenate([edge_flat, ocean_state[send_tile].reshape(-1)])
+
+    both_states = jnp.concatenate([atmos_state, ocean_state], axis=1)
+    edges_cm = pick(edge_matrix(), both_states, "qe,bcq->cbe")
+    sea_here = lax.dynamic_slice_in_dim(sea_mask, first_tile, per_dev, 0).astype(jnp.bfloat16)
+    edges_cm = jnp.concatenate(
+        [edges_cm[:atmos_local], edges_cm[atmos_local:] * sea_here[None, :, None]], axis=0
+    )
+    edge_flat = edges_cm.reshape(-1)
+    edge_size = edge_flat.shape[0]
+    outgoing = jnp.concatenate([edge_flat, ocean_state.reshape(-1)])
     from_left = lax.ppermute(outgoing, "tiles", [(i, (i + 1) % groups) for i in range(groups)])
     from_right = lax.ppermute(outgoing, "tiles", [((i + 1) % groups, i) for i in range(groups)])
-    edge_size = edge_flat.shape[0]
-    partner_ocean = jnp.where(parity == 0, from_right[edge_size:], from_left[edge_size:])
-    own_ocean = jnp.where(
-        from_here[:, None, None],
-        ocean_state[own_tile],
-        partner_ocean.reshape((per_owner,) + ocean_state.shape[1:]),
-    )
-    widened = jnp.concatenate(
-        [from_left[:edge_size], edge_flat, from_right[:edge_size]]
-    )
-    widened = widened.reshape(3 * per_dev, atmos_local + ocean_local, 4, SIDE)
+
+    sea_count = jnp.cumsum(sea_mask)
+    pair_base = tile_group // 2 * 2 * per_owner
+    ranks_own = pair_base + 2 * jnp.arange(per_owner, dtype=jnp.int32) + parity
+    tiles_own = jnp.sum((sea_count[None, :] <= ranks_own[:, None]).astype(jnp.int32), axis=1)
+    pair_index = tiles_own - tile_group // 2 * 2 * per_dev
+    own_pick = (
+        pair_index[:, None] == jnp.arange(2 * per_dev, dtype=jnp.int32)[None, :]
+    ).astype(jnp.bfloat16)
+
     adjacent = lax.dynamic_slice_in_dim(neighbours, first_tile, per_dev, 0)
     turn_codes = lax.dynamic_slice_in_dim(rotations, first_tile, per_dev, 0)
     local_adjacent = (adjacent // per_dev - tile_group + 1) % groups * per_dev + adjacent % per_dev
-    rim_cells = pick_rims(widened, local_adjacent, turn_codes)
-    rims_cm = jnp.transpose(rim_cells, (2, 0, 1, 3)).reshape(
-        atmos_local + ocean_local, per_dev, 4 * SIDE
-    )
+    tile_hit = local_adjacent[None, None, :, :] == jnp.arange(3 * per_dev, dtype=jnp.int32)[
+        :, None, None, None
+    ]
+    edge_hit = (turn_codes % 4)[None, None, :, :] == jnp.arange(4, dtype=jnp.int32)[
+        None, :, None, None
+    ]
+    rim_pick = (tile_hit & edge_hit).astype(jnp.bfloat16).reshape(3 * per_dev * 4, per_dev * 4)
+    flip = (
+        lax.broadcasted_iota(jnp.int32, (SIDE, SIDE), 0)
+        == SIDE - 1 - lax.broadcasted_iota(jnp.int32, (SIDE, SIDE), 1)
+    ).astype(jnp.bfloat16)
+
+    partner_state = jnp.where(parity == 0, from_right[edge_size:], from_left[edge_size:])
+    pair_state = pair_order(ocean_state, partner_state.reshape(ocean_state.shape), parity)
+    ocean_cm = pick(own_pick, pair_state, "st,tcp->csp")
+    own_ocean = pick(own_pick, pair_state, "st,tcp->scp")
+
+    widened = jnp.concatenate(
+        [
+            from_left[:edge_size].reshape(edges_cm.shape),
+            edges_cm,
+            from_right[:edge_size].reshape(edges_cm.shape),
+        ],
+        axis=1,
+    ).reshape(chans, 3 * per_dev * 4, SIDE)
+    straight = pick(rim_pick, widened, "xy,cxk->cyk")
+    turned = pick(flip, straight, "kj,cyk->cyj")
+    reverse = (turn_codes >= 4).reshape(-1)
+    rims_cm = jnp.where(reverse[None, :, None], turned, straight).reshape(chans, per_dev, 4 * SIDE)
 
     early = 2 * SIDE
-    pixels = SIDE * SIDE
-    ocean_cm = jnp.transpose(own_ocean, (1, 0, 2))
     atmos_int, atmos_rims, ocean_head = gather_rows(
         [jnp.transpose(atmos_state, (1, 0, 2)), rims_cm[:atmos_local], ocean_cm[:, :, :early]]
     )
@@ -217,19 +254,21 @@
         atmos_state.astype(jnp.float32) + jax.nn.gelu(trim_columns(atmos_accum), approximate=True)
     ).astype(jnp.bfloat16)
 
-    sea_width = ocean_local * 4 * SIDE
+    sea_rims = jnp.transpose(rims_cm[atmos_local:], (1, 0, 2))
     late_block = jnp.concatenate(
-        [atmos_next.reshape(per_dev, -1), rim_cells[:, :, atmos_local:].reshape(per_dev, -1)], axis=1
-    )
-    late_own = jnp.where(
-        from_here[:, None], late_block[own_tile], partner(late_block[send_tile], "tiles", 0)
-    )
-    forcing = late_own[:, : late_block.shape[1] - sea_width].reshape(per_owner, atmos_local, pixels)
-    own_rims = late_own[:, late_block.shape[1] - sea_width :].reshape(per_owner, 4, ocean_local, SIDE)
-    own_rims = jnp.transpose(own_rims, (2, 0, 1, 3)).reshape(ocean_local, per_owner, 4 * SIDE)
+        [atmos_next.reshape(per_dev, -1), sea_rims.reshape(per_dev, -1)], axis=1
+    )
+    pair_late = pair_order(late_block, partner(late_block, "tiles", 0), parity)
+    force_width = atmos_local * pixels
+    forcing_cm = pick(
+        own_pick, pair_late[:, :force_width].reshape(2 * per_dev, atmos_local, pixels), "st,tcp->csp"
+    )
+    own_rims_cm = pick(
+        own_pick, pair_late[:, force_width:].reshape(2 * per_dev, ocean_local, 4 * SIDE), "st,tcp->csp"
+    )
 
     ocean_tail, ocean_rims, force_all = gather_rows(
-        [ocean_cm[:, :, early:], own_rims, jnp.transpose(forcing, (1, 0, 2))]
+        [ocean_cm[:, :, early:], own_rims_cm, forcing_cm]
     )
     ocean_pad = placed(
         [

time: 96.1 us -> 89.3 us (0.929)
  local copies, waits for them, and re-layouts: 20 us -> 14.9 us
  other arithmetic: 6.68 us -> 5 us
  matrix products: 6.76 us -> 7.84 us
    gather x5 -> x0, local copies, waits for them, and re-layouts: 3.66 us -> none  [the longest x1 1.31 us: local(): outgoing = jnp.concatenate([edge_flat, ocean_state[send_tile].reshape(-1)])]
    transpose x0 -> x2, local copies, waits for them, and re-layouts: none -> 1.97 us  [the longest x1 1.96 us: conv_cm(): jnp.einsum('kc,bcp->bkp', weight.reshape(taps * out_chans, in_chans), pad...]
    dot_general x1 -> x0, local copies, waits for them, and re-layouts: 1.96 us -> none  [conv_cm(): jnp.einsum('kc,cbp->kbp', weight.reshape(taps * out_chans, in_chans), pad...]
    dot_general x5 -> x12, matrix products: 5.93 us -> 7.64 us  [the longest x2 4.02 us: conv_cm(): jnp.einsum('kc,bcp->bkp', weight.reshape(taps * out_chans, in_chans), pad...]
    add x3, other arithmetic: 1.67 us -> 0.02 us  [interior_spots(): return (pixel // SIDE + 1) * (SIDE + 2) + pixel % SIDE + 1]
    ppermute x1, waiting for transfers between devices: 1.38 us -> 0.01 us  [local(): lax.ppermute(outgoing, 'tiles', [(i, (i + 1) % groups) for i in range(gro...]
    concatenate x6 -> x3, local copies, waits for them, and re-layouts: 1.2 us -> 0.03 us  [the longest x1 0.02 us: local(): jnp.concatenate([from_left[:edge_size].reshape(edges_cm.shape), edges_cm,...]
    unnamed x46 -> x25, local copies, waits for them, and re-layouts: 4.09 us -> 4.69 us
  transfers between devices with their start and end apart: 3 -> 3, of which waited for: 1 -> 1; matrix products, arithmetic and copies ran while one was open for 5% -> 7% of each run, Pallas kernels for 0% -> 0%
where the time goes in v4:
time: 89.3 us; the launch traced here: 88.3 us
  blocking collectives  47.8 us (54%)
  local copies, waits for them, and re-layouts  14.9 us (17%)
  starting transfers between devices  10.9 us (12%)
  matrix products  7.84 us (9%)
  other arithmetic  5 us (6%)
  between operations  1.27 us (1%)
    all_gather x2, blocking collectives, gather_rows(): gathered = lax.all_gather(rows, 'chan', axis=0, tiled=False)  47.8 us
    ppermute x1, starting transfers between devices, local(): lax.ppermute(outgoing, 'tiles', [((i + 1) % groups, i) for i in range(gro...  8.95 us
    unnamed x25, local copies, waits for them, and re-layouts  4.69 us
    dot_general x2, matrix products, conv_cm(): jnp.einsum('kc,bcp->bkp', weight.reshape(taps * out_chans, in_chans), pad...  4.02 us
    reshape x6, local copies, waits for them, and re-layouts, gather_rows(): parts.append(part.reshape((groups * piece.shape[0],) + piece.shape[1:]))  3.56 us
    dot_general x7, matrix products, pick(): jnp.einsum(spec, selector, values, preferred_element_type=jnp.float32)  2.25 us
    transpose x1, local copies, waits for them, and re-layouts, conv_cm(): jnp.einsum('kc,bcp->bkp', weight.reshape(taps * out_chans, in_chans), pad...  1.96 us
    ppermute x1, starting transfers between devices, partner(): return lax.ppermute(value, axis, pairs)  1.92 us
  transfers between devices with their start and end apart: 3, of which 1 were waited for; matrix products, arithmetic and copies ran while one was open for 7% of the time, Pallas kernels for 0%

profile of v4, /device:TPU:6, one launch (start us, length us, event | category | flops | bytes accessed | tf_op | source)
XLA Modules:
  0.0 88.3 jit_solution(7681389383311194436)
XLA Ops:
  0.7 0.8 copy.222
  1.5 0.8 copy.171
  2.4 1.0 %fusion.9 = bf16[20,8,64]{2,0,1:T(8,128)(2,1)S(1)} fusion(bf16[8,8,256]{2,1,0:T(8,128)(2,1)} %param.9, bf16[8,12,256]{2,1,0:T(8,128)(2,1)S(1)} %copy.171, s32[64]{0:T(128)S(1)} %pad_add_fusion), kind=kOutput, calls=%fused_computation.20 | convolution fusion | flops 5433344 | bytes 102656 | tf_op jit(solution)/shard_map/qe,bcq->cbe/dot_general | solution.py:154
  3.4 0.8 dynamic-slice_convert_fusion
  4.4 8.9 %collective-permute-start.1 = (bf16[26624]{0:T(1024)(128)(2,1)S(1)}, bf16[26624]{0:T(1024)(128)(2,1)S(1)}, u32[]{:S(2)}, u32[]{:S(2)}) collective-permute-start(bf16[26624]{0:T(1024)(128)(2,1)S(1)} %constant_dynamic-update-slice_fusion), channel_id=1, source_target_pairs={{16,0},{32,16},{48,32},{64,48},{80,64},{96,80},{112,96},{128,112},... | collective-permute-start | bytes 159752 | tf_op jit(solution)/shard_map/ppermute | solution.py:203
  13.4 0.8 dynamic-slice_compare_fusion
  14.2 1.0 %reduce-window.9 = s32[2,128]{1,0:T(2,128)S(1)} reduce-window(s32[2,128]{1,0:T(2,128)} %bitcast.177, s32[]{:T(128)} %constant.167.clone.1), window={size=1x128 pad=0_0x127_0}, to_apply=%region_0.1 | reduce-window | flops 32512 | bytes 2052 | tf_op jit(solution)/shard_map/reduce-window
  15.5 0.8 add_select_fusion
  17.3 0.8 copy.221
  18.1 0.9 %reshape.319 = bf16[108,192]{1,0:T(8,128)(2,1)S(1)} reshape(bf16[9,12,192]{2,1,0:T(8,128)(2,1)} %param.10) | data formatting | bytes 82944 | tf_op jit(solution)/shard_map/reshape | solution.py:141
  21.4 24.7 %all_gather.6 = bf16[16,126,256]{2,1,0:T(8,128)(2,1)S(1)} all-gather(bf16[1,126,256]{2,1,0:T(8,128)(2,1)S(1)} %all_gather_reshape.6), channel_id=1, replica_groups=mesh['tiles'=32,'chan'=16] {'chan'}, dimensions={0}, use_global_device_ids=true | all-gather | bytes 1096704 | tf_op jit(solution)/shard_map/all_gather | solution.py:94
  46.1 0.6 copy.223
  47.5 1.1 %reshape.318 = bf16[192,8,64]{2,1,0:T(8,128)(2,1)} reshape(bf16[16,6144]{1,0:T(8,128)(2,1)S(1)} %slice.207) | data formatting | bytes 393216 | tf_op jit(solution)/shard_map/reshape | solution.py:102
  48.8 0.6 fusion.12
  49.4 3.3 %convolution_bitcast_fusion = f32[8,108,326]{1,2,0:T(8,128)} fusion(f32[326,192,8]{0,1,2:T(8,128)S(1)} %fusion.12, bf16[192,8,64]{2,1,0:T(8,128)(2,1)} %reshape.318, bf16[108,192]{1,0:T(8,128)(2,1)S(1)} %reshape.319, s32[64]{0:T(128)S(1)} %pad_add_fusion.1), kind=kOutput, calls=%fused_computation.1 | convolution fusion | flops 173275520 | bytes 3367936 | tf_op jit(solution)/shard_map/kc,bcp->bkp/dot_general | solution.py:139
  52.7 2.0 %copy.187 = f32[8,108,326]{2,0,1:T(8,128)S(1)} copy(f32[8,108,326]{1,2,0:T(8,128)} %convolution_bitcast_fusion) | data formatting | bytes 2253312 | tf_op jit(solution)/shard_map/kc,bcp->bkp/transpose | solution.py:139
  56.0 1.9 %collective-permute-start.2 = (bf16[8,3584]{1,0:T(8,128)(2,1)S(1)}, bf16[8,3584]{1,0:T(8,128)(2,1)S(1)}, u32[]{:S(2)}, u32[]{:S(2)}) collective-permute-start(bf16[8,3584]{1,0:T(8,128)(2,1)S(1)} %pad_maximum_fusion.5), channel_id=1, source_target_pairs={{0,16},{16,0},{32,48},{48,32},{64,80},{80,64},{96,112},{112,96},{1... | collective-permute-start | bytes 172040 | tf_op jit(solution)/shard_map/ppermute | solution.py:28
  58.5 0.6 collective-permute-done.2
  59.8 23.1 %all_gather.7 = bf16[16,126,256]{2,1,0:T(8,128)(2,1)S(1)} all-gather(bf16[1,126,256]{2,1,0:T(8,128)(2,1)S(1)} %all_gather_reshape.7), channel_id=1, replica_groups=mesh['tiles'=32,'chan'=16] {'chan'}, dimensions={0}, use_global_device_ids=true | all-gather | bytes 1096704 | tf_op jit(solution)/shard_map/all_gather | solution.py:94
  82.9 0.6 copy.224
  83.8 0.8 reshape.331
  85.0 0.7 convolution_bitcast_fusion.1
  86.0 0.9 %reshape.336 = bf16[192,6,256]{2,1,0:T(8,128)(2,1)S(1)} reshape(bf16[16,18432]{1,0:T(8,128)(2,1)S(1)} %slice.233) | data formatting | bytes 1179648 | tf_op jit(solution)/shard_map/reshape | solution.py:102
  87.7 0.6 copy.207
  (114 shorter events, 8.9 us)
Async XLA Ops:
  0.6 84.3 %copy-start = (bf16[9,8,128]{2,1,0:T(8,128)(2,1)S(1)}, bf16[9,8,128]{2,1,0:T(8,128)(2,1)}, u32[]{:S(2)}) copy-start(bf16[9,8,128]{2,1,0:T(8,128)(2,1)} %param.11) | copy-start | bytes 55300
  0.6 19.7 %copy-start.3 = (bf16[8,8,256]{2,1,0:T(8,128)(2,1)S(1)}, bf16[8,8,256]{2,1,0:T(8,128)(2,1)}, u32[]{:S(2)}) copy-start(bf16[8,8,256]{2,1,0:T(8,128)(2,1)} %param.9) | copy-start | bytes 98308
  4.4 14.8 %collective-permute-start.1 = (bf16[26624]{0:T(1024)(128)(2,1)S(1)}, bf16[26624]{0:T(1024)(128)(2,1)S(1)}, u32[]{:S(2)}, u32[]{:S(2)}) collective-permute-start(bf16[26624]{0:T(1024)(128)(2,1)S(1)} %constant_dynamic-update-slice_fusion), channel_id=1, source_target_pairs={{16,0},{32,16},{48,32},{64,48},{80,64},{96,80},{112,96},{128,112},... | collective-permute-start | bytes 159752 | tf_op jit(solution)/shard_map/ppermute | solution.py:203
  13.4 6.0 %collective-permute-start = (bf16[26624]{0:T(1024)(128)(2,1)S(1)}, bf16[26624]{0:T(1024)(128)(2,1)S(1)}, u32[]{:S(2)}, u32[]{:S(2)}) collective-permute-start(bf16[26624]{0:T(1024)(128)(2,1)S(1)} %constant_dynamic-update-slice_fusion), channel_id=1, source_target_pairs={{0,16},{16,32},{32,48},{48,64},{64,80},{80,96},{96,112},{112,128},... | collective-permute-start | bytes 159752 | tf_op jit(solution)/shard_map/ppermute | solution.py:202
  20.4 0.6 copy-start.4
  20.4 26.3 %copy-start.6 = (bf16[8,8,256]{2,0,1:T(8,128)(2,1)}, bf16[8,8,256]{2,0,1:T(8,128)(2,1)S(1)}, u32[]{:S(2)}) copy-start(bf16[8,8,256]{2,0,1:T(8,128)(2,1)S(1)} %get-tuple-element.17) | copy-start | bytes 98308
  52.7 3.2 %copy-start.1 = (bf16[8,12,256]{2,0,1:T(8,128)(2,1)S(1)}, bf16[8,12,256]{2,0,1:T(8,128)(2,1)}, u32[]{:S(2)}) copy-start(bf16[8,12,256]{2,0,1:T(8,128)(2,1)} %param.8) | copy-start | bytes 147460
  56.0 27.6 %copy-start.2 = (bf16[8,12,256]{2,0,1:T(8,128)(2,1)}, bf16[8,12,256]{2,0,1:T(8,128)(2,1)S(1)}, u32[]{:S(2)}) copy-start(bf16[8,12,256]{2,0,1:T(8,128)(2,1)S(1)} %fusion.37) | copy-start | bytes 147460
  56.0 3.1 %collective-permute-start.2 = (bf16[8,3584]{1,0:T(8,128)(2,1)S(1)}, bf16[8,3584]{1,0:T(8,128)(2,1)S(1)}, u32[]{:S(2)}, u32[]{:S(2)}) collective-permute-start(bf16[8,3584]{1,0:T(8,128)(2,1)S(1)} %pad_maximum_fusion.5), channel_id=1, source_target_pairs={{0,16},{16,0},{32,48},{48,32},{64,80},{80,64},{96,112},{112,96},{1... | collective-permute-start | bytes 172040 | tf_op jit(solution)/shard_map/ppermute | solution.py:28
  85.0 2.3 %copy-start.8 = (bf16[8,192]{1,0:T(8,128)(2,1)S(1)}, bf16[8,192]{1,0:T(8,128)(2,1)}, u32[]{:S(2)}) copy-start(bf16[8,192]{1,0:T(8,128)(2,1)} %param.12) | copy-start | bytes 9220
  85.0 2.5 %copy-start.5 = (bf16[8,8,256]{2,0,1:T(8,128)(2,1)S(1)}, bf16[8,8,256]{2,0,1:T(8,128)(2,1)}, u32[]{:S(2)}) copy-start(bf16[8,8,256]{2,0,1:T(8,128)(2,1)} %copy-done.4) | copy-start | bytes 98308
  85.0 2.5 %copy-start.7 = (bf16[8,8,256]{2,0,1:T(8,128)(2,1)S(1)}, bf16[8,8,256]{2,0,1:T(8,128)(2,1)}, u32[]{:S(2)}) copy-start(bf16[8,8,256]{2,0,1:T(8,128)(2,1)} %copy-done.6) | copy-start | bytes 98308

commit v5 on v4

--- a/solution.py
+++ b/solution.py
@@ -125,7 +125,7 @@
     total = None
     for piece, spots in pieces:
         term = jnp.einsum(
-            "cbq,qp->bcp", piece, place_matrix(spots, width), preferred_element_type=jnp.float32
+            "cbq,qp->cbp", piece, place_matrix(spots, width), preferred_element_type=jnp.float32
         )
         total = term if total is None else total + term
     return total.astype(jnp.bfloat16)
@@ -134,20 +134,13 @@
 def conv_cm(weight, padded):
     row_width = SIDE + 2
     out_span = SIDE * row_width
-    taps, out_chans, in_chans = weight.shape
-    tile_count = padded.shape[0]
-    products = jnp.einsum(
-        "kc,bcp->bkp",
-        weight.reshape(taps * out_chans, in_chans),
-        padded,
-        preferred_element_type=jnp.float32,
-    ).reshape(tile_count, taps, out_chans, padded.shape[2])
+    products = jnp.einsum("toc,cbp->tobp", weight, padded, preferred_element_type=jnp.float32)
     accum = None
-    for tap_index in range(taps):
+    for tap_index in range(weight.shape[0]):
         offset = tap_index // 3 * row_width + tap_index % 3
-        term = products[:, tap_index, :, offset : offset + out_span]
+        term = products[tap_index, :, :, offset : offset + out_span]
         accum = term if accum is None else accum + term
-    return accum
+    return jnp.transpose(accum, (1, 0, 2))
 
 
 def pick(selector, values, spec):
@@ -192,7 +185,10 @@
 
     both_states = jnp.concatenate([atmos_state, ocean_state], axis=1)
     edges_cm = pick(edge_matrix(), both_states, "qe,bcq->cbe")
-    sea_here = lax.dynamic_slice_in_dim(sea_mask, first_tile, per_dev, 0).astype(jnp.bfloat16)
+    tables = lax.dynamic_slice_in_dim(
+        jnp.concatenate([neighbours, rotations, sea_mask[:, None]], axis=1), first_tile, per_dev, 0
+    )
+    sea_here = tables[:, 8].astype(jnp.bfloat16)
     edges_cm = jnp.concatenate(
         [edges_cm[:atmos_local], edges_cm[atmos_local:] * sea_here[None, :, None]], axis=0
     )
@@ -202,17 +198,22 @@
     from_left = lax.ppermute(outgoing, "tiles", [(i, (i + 1) % groups) for i in range(groups)])
     from_right = lax.ppermute(outgoing, "tiles", [((i + 1) % groups, i) for i in range(groups)])
 
-    sea_count = jnp.cumsum(sea_mask)
-    pair_base = tile_group // 2 * 2 * per_owner
-    ranks_own = pair_base + 2 * jnp.arange(per_owner, dtype=jnp.int32) + parity
-    tiles_own = jnp.sum((sea_count[None, :] <= ranks_own[:, None]).astype(jnp.int32), axis=1)
-    pair_index = tiles_own - tile_group // 2 * 2 * per_dev
+    pair_tiles = 2 * per_dev
+    pair_first = tile_group // 2 * pair_tiles
+    pair_mask = lax.dynamic_slice_in_dim(sea_mask, pair_first, pair_tiles, 0)
+    upto = (
+        lax.broadcasted_iota(jnp.int32, (pair_tiles, pair_tiles), 1)
+        <= lax.broadcasted_iota(jnp.int32, (pair_tiles, pair_tiles), 0)
+    )
+    pair_count = jnp.sum(jnp.where(upto, pair_mask[None, :], 0), axis=1)
+    local_rank = 2 * jnp.arange(per_owner, dtype=jnp.int32) + parity
+    pair_index = jnp.sum((pair_count[None, :] <= local_rank[:, None]).astype(jnp.int32), axis=1)
     own_pick = (
-        pair_index[:, None] == jnp.arange(2 * per_dev, dtype=jnp.int32)[None, :]
+        pair_index[:, None] == jnp.arange(pair_tiles, dtype=jnp.int32)[None, :]
     ).astype(jnp.bfloat16)
 
-    adjacent = lax.dynamic_slice_in_dim(neighbours, first_tile, per_dev, 0)
-    turn_codes = lax.dynamic_slice_in_dim(rotations, first_tile, per_dev, 0)
+    adjacent = tables[:, :4]
+    turn_codes = tables[:, 4:8]
     local_adjacent = (adjacent // per_dev - tile_group + 1) % groups * per_dev + adjacent % per_dev
     tile_hit = local_adjacent[None, None, :, :] == jnp.arange(3 * per_dev, dtype=jnp.int32)[
         :, None, None, None

time: 89.3 us -> 90.6 us (1.015)
  waiting for transfers between devices: 0.59 us -> 1.81 us
    transpose x0 -> x1, other arithmetic: none -> 2 us  [conv_cm(): return jnp.transpose(accum, (1, 0, 2))]
    transpose x1, local copies, waits for them, and re-layouts: 1.96 us -> 0.05 us  [conv_cm(): return jnp.transpose(accum, (1, 0, 2))]
    ppermute x1, waiting for transfers between devices: 0.01 us -> 1.2 us  [local(): lax.ppermute(outgoing, 'tiles', [(i, (i + 1) % groups) for i in range(gro...]
    another operation x3 -> x0, other arithmetic: 1.09 us -> none
    reshape x1 -> x0, local copies, waits for them, and re-layouts: 0.91 us -> none  [conv_cm(): weight.reshape(taps * out_chans, in_chans)]
    unnamed x25 -> x38, local copies, waits for them, and re-layouts: 4.69 us -> 4.69 us
  transfers between devices with their start and end apart: 3 -> 3, of which waited for: 1 -> 2; matrix products, arithmetic and copies ran while one was open for 7% -> 5% of each run, Pallas kernels for 0% -> 0%
where the time goes in v5:
time: 90.6 us; the launch traced here: 89.6 us
  blocking collectives  47.9 us (53%)
  local copies, waits for them, and re-layouts  14.1 us (16%)
  starting transfers between devices  10.9 us (12%)
  matrix products  7.78 us (9%)
  other arithmetic  5.82 us (6%)
  waiting for transfers between devices  1.81 us (2%)
  between operations  1.34 us (1%)
    all_gather x2, blocking collectives, gather_rows(): gathered = lax.all_gather(rows, 'chan', axis=0, tiled=False)  47.9 us
    ppermute x1, starting transfers between devices, local(): lax.ppermute(outgoing, 'tiles', [((i + 1) % groups, i) for i in range(gro...  8.95 us
    unnamed x38, local copies, waits for them, and re-layouts  4.69 us
    dot_general x2, matrix products, conv_cm(): jnp.einsum('toc,cbp->tobp', weight, padded, preferred_element_type=jnp.fl...  3.97 us
    reshape x6, local copies, waits for them, and re-layouts, gather_rows(): parts.append(part.reshape((groups * piece.shape[0],) + piece.shape[1:]))  3.57 us
    dot_general x7, matrix products, pick(): jnp.einsum(spec, selector, values, preferred_element_type=jnp.float32)  2.25 us
    transpose x1, other arithmetic, conv_cm(): return jnp.transpose(accum, (1, 0, 2))  2 us
    ppermute x1, starting transfers between devices, partner(): return lax.ppermute(value, axis, pairs)  1.92 us
  transfers between devices with their start and end apart: 3, of which 2 were waited for; matrix products, arithmetic and copies ran while one was open for 5% of the time, Pallas kernels for 0%

profile of v5, /device:TPU:6, one launch (start us, length us, event | category | flops | bytes accessed | tf_op | source)
XLA Modules:
  0.0 89.6 jit_solution(18106454149987285287)
XLA Ops:
  0.7 0.8 fusion.71
  1.5 0.8 copy.169
  2.3 0.8 copy.135
  3.2 1.0 %fusion.9 = bf16[20,8,64]{2,0,1:T(8,128)(2,1)S(1)} fusion(bf16[8,8,256]{2,1,0:T(8,128)(2,1)} %param.9, bf16[8,12,256]{2,1,0:T(8,128)(2,1)S(1)} %copy.135, s32[64]{0:T(128)S(1)} %get-tuple-element.20), kind=kOutput, calls=%fused_computation.20 | convolution fusion | flops 5433344 | bytes 102656 | tf_op jit(solution)/shard_map/qe,bcq->cbe/dot_general | solution.py:147
  4.5 8.9 %collective-permute-start.1 = (bf16[26624]{0:T(1024)(128)(2,1)S(1)}, bf16[26624]{0:T(1024)(128)(2,1)S(1)}, u32[]{:S(2)}, u32[]{:S(2)}) collective-permute-start(bf16[26624]{0:T(1024)(128)(2,1)S(1)} %constant_dynamic-update-slice_fusion), channel_id=1, source_target_pairs={{16,0},{32,16},{48,32},{64,48},{80,64},{96,80},{112,96},{128,112},... | collective-permute-start | bytes 159752 | tf_op jit(solution)/shard_map/ppermute | solution.py:199
  14.0 0.8 dynamic_slice.7
  15.8 0.8 copy.168
  17.0 1.2 %collective-permute-done = bf16[26624]{0:T(1024)(128)(2,1)S(1)} collective-permute-done((bf16[26624]{0:T(1024)(128)(2,1)S(1)}, bf16[26624]{0:T(1024)(128)(2,1)S(1)}, u32[]{:S(2)}, u32[]{:S(2)}) %collective-permute-start) | collective-permute-done | bytes 53280 | tf_op jit(solution)/shard_map/ppermute | solution.py:198
  20.2 24.7 %all_gather.6 = bf16[16,126,256]{2,1,0:T(8,128)(2,1)S(1)} all-gather(bf16[1,126,256]{2,1,0:T(8,128)(2,1)S(1)} %all_gather_reshape.6), channel_id=1, replica_groups=mesh['tiles'=32,'chan'=16] {'chan'}, dimensions={0}, use_global_device_ids=true | all-gather | bytes 1096704 | tf_op jit(solution)/shard_map/all_gather | solution.py:94
  45.6 0.7 slice-done
  47.0 1.2 %reshape.270 = bf16[192,8,64]{2,1,0:T(8,128)(2,1)} reshape(bf16[16,6144]{1,0:T(8,128)(2,1)S(1)} %slice.214) | data formatting | bytes 393216 | tf_op jit(solution)/shard_map/reshape | solution.py:102
  48.3 0.6 fusion.12
  49.0 3.2 %convolution_bitcast_fusion = f32[9,12,8,326]{3,1,0,2:T(8,128)} fusion(f32[192,8,326]{2,0,1:T(8,128)S(1)} %fusion.12, bf16[192,8,64]{2,1,0:T(8,128)(2,1)} %reshape.270, bf16[9,12,192]{2,1,0:T(8,128)(2,1)S(1)} %copy-done, s32[64]{0:T(128)S(1)} %get-tuple-element.21), kind=kOutput, calls=%fused_computation.1 | convolution fusion | flops 173275520 | bytes 3367936 | tf_op jit(solution)/shard_map/toc,cbp->tobp/dot_general | solution.py:137
  52.2 2.0 %fusion.23 = f32[8,12,288]{2,1,0:T(8,128)S(1)} fusion(f32[9,12,8,326]{3,1,0,2:T(8,128)} %convolution_bitcast_fusion), kind=kLoop, calls=%fused_computation.35 | loop fusion | flops 221184 | bytes 1105920 | tf_op jit(solution)/shard_map/transpose | solution.py:143
  55.2 1.9 %collective-permute-start.2 = (bf16[8,3584]{1,0:T(8,128)(2,1)S(1)}, bf16[8,3584]{1,0:T(8,128)(2,1)S(1)}, u32[]{:S(2)}, u32[]{:S(2)}) collective-permute-start(bf16[8,3584]{1,0:T(8,128)(2,1)S(1)} %pad_maximum_fusion.5), channel_id=1, source_target_pairs={{0,16},{16,0},{32,48},{48,32},{64,80},{80,64},{96,112},{112,96},{1... | collective-permute-start | bytes 172040 | tf_op jit(solution)/shard_map/ppermute | solution.py:28
  57.7 0.6 collective-permute-done.2
  59.0 23.1 %all_gather.7 = bf16[16,126,256]{2,1,0:T(8,128)(2,1)S(1)} all-gather(bf16[1,126,256]{2,1,0:T(8,128)(2,1)S(1)} %all_gather_reshape.7), channel_id=1, replica_groups=mesh['tiles'=32,'chan'=16] {'chan'}, dimensions={0}, use_global_device_ids=true | all-gather | bytes 1096704 | tf_op jit(solution)/shard_map/all_gather | solution.py:94
  82.2 0.6 copy.171
  82.8 0.9 slice.240
  83.9 0.8 reshape.282
  85.0 0.7 convolution_bitcast_fusion.1
  85.8 1.4 %slice_add_fusion.8 = f32[1,8,6,288]{3,0,1,2:T(1,128)S(1)} fusion(f32[9,8,6,326]{3,0,1,2:T(8,128)S(1)} %convolution_bitcast_fusion.1), kind=kLoop, calls=%fused_computation.69 | loop fusion | flops 110592 | bytes 552960 | tf_op jit(solution)/shard_map/add | solution.py:142
  87.2 0.9 %reshape.286 = bf16[192,6,256]{2,1,0:T(8,128)(2,1)S(1)} reshape(bf16[16,18432]{1,0:T(8,128)(2,1)S(1)} %copy-done.1) | data formatting | bytes 1179648 | tf_op jit(solution)/shard_map/reshape | solution.py:102
  89.0 0.6 copy.162
  (126 shorter events, 9.3 us)
Async XLA Ops:
  0.6 48.3 %copy-start = (bf16[9,12,192]{2,1,0:T(8,128)(2,1)S(1)}, bf16[9,12,192]{2,1,0:T(8,128)(2,1)}, u32[]{:S(2)}) copy-start(bf16[9,12,192]{2,1,0:T(8,128)(2,1)} %param.10) | copy-start | bytes 124420
  4.2 15.0 %copy-start.5 = (bf16[8,8,256]{2,1,0:T(8,128)(2,1)S(1)}, bf16[8,8,256]{2,1,0:T(8,128)(2,1)}, u32[]{:S(2)}) copy-start(bf16[8,8,256]{2,1,0:T(8,128)(2,1)} %param.9) | copy-start | bytes 98308
  4.5 12.4 %collective-permute-start.1 = (bf16[26624]{0:T(1024)(128)(2,1)S(1)}, bf16[26624]{0:T(1024)(128)(2,1)S(1)}, u32[]{:S(2)}, u32[]{:S(2)}) collective-permute-start(bf16[26624]{0:T(1024)(128)(2,1)S(1)} %constant_dynamic-update-slice_fusion), channel_id=1, source_target_pairs={{16,0},{32,16},{48,32},{64,48},{80,64},{96,80},{112,96},{128,112},... | collective-permute-start | bytes 159752 | tf_op jit(solution)/shard_map/ppermute | solution.py:199
  13.4 4.8 %collective-permute-start = (bf16[26624]{0:T(1024)(128)(2,1)S(1)}, bf16[26624]{0:T(1024)(128)(2,1)S(1)}, u32[]{:S(2)}, u32[]{:S(2)}) collective-permute-start(bf16[26624]{0:T(1024)(128)(2,1)S(1)} %constant_dynamic-update-slice_fusion), channel_id=1, source_target_pairs={{0,16},{16,32},{32,48},{48,64},{64,80},{80,96},{96,112},{112,128},... | collective-permute-start | bytes 159752 | tf_op jit(solution)/shard_map/ppermute | solution.py:198
  15.4 43.3 %copy-start.12 = (s32[6]{0:T(128)}, s32[6]{0:T(128)S(1)}, u32[]{:S(2)}) copy-start(s32[6]{0:T(128)S(1)} %convert_reduce_fusion) | copy-start | bytes 76
  19.1 26.4 %copy-start.4 = (bf16[20,32,16]{1,2,0:T(8,128)(2,1)}, bf16[20,32,16]{1,2,0:T(8,128)(2,1)S(1)}, u32[]{:S(2)}) copy-start(bf16[20,32,16]{1,2,0:T(8,128)(2,1)S(1)} %fusion.3) | copy-start | bytes 61444
  19.2 0.6 copy-start.7
  19.2 26.3 %copy-start.9 = (bf16[8,8,256]{2,0,1:T(8,128)(2,1)}, bf16[8,8,256]{2,0,1:T(8,128)(2,1)S(1)}, u32[]{:S(2)}) copy-start(bf16[8,8,256]{2,0,1:T(8,128)(2,1)S(1)} %get-tuple-element.17) | copy-start | bytes 98308
  45.5 0.8 slice-start
  52.2 2.9 %copy-start.2 = (bf16[8,12,256]{2,0,1:T(8,128)(2,1)S(1)}, bf16[8,12,256]{2,0,1:T(8,128)(2,1)}, u32[]{:S(2)}) copy-start(bf16[8,12,256]{2,0,1:T(8,128)(2,1)} %param.8) | copy-start | bytes 147460
  55.1 27.0 %copy-start.3 = (bf16[8,12,256]{2,0,1:T(8,128)(2,1)}, bf16[8,12,256]{2,0,1:T(8,128)(2,1)S(1)}, u32[]{:S(2)}) copy-start(bf16[8,12,256]{2,0,1:T(8,128)(2,1)S(1)} %fusion.38) | copy-start | bytes 147460
  55.2 3.1 %collective-permute-start.2 = (bf16[8,3584]{1,0:T(8,128)(2,1)S(1)}, bf16[8,3584]{1,0:T(8,128)(2,1)S(1)}, u32[]{:S(2)}, u32[]{:S(2)}) collective-permute-start(bf16[8,3584]{1,0:T(8,128)(2,1)S(1)} %pad_maximum_fusion.5), channel_id=1, source_target_pairs={{0,16},{16,0},{32,48},{48,32},{64,80},{80,64},{96,112},{112,96},{1... | collective-permute-start | bytes 172040 | tf_op jit(solution)/shard_map/ppermute | solution.py:28
  82.7 1.9 %copy-start.11 = (s32[224]{0:T(256)S(1)}, s32[224]{0:T(256)}, u32[]{:S(2)}) copy-start(s32[224]{0:T(256)} %fusion.99) | copy-start | bytes 2692
  83.7 1.4 %copy-start.6 = (bf16[9,8,128]{2,1,0:T(8,128)(2,1)S(1)}, bf16[9,8,128]{2,1,0:T(8,128)(2,1)}, u32[]{:S(2)}) copy-start(bf16[9,8,128]{2,1,0:T(8,128)(2,1)} %param.11) | copy-start | bytes 55300
  85.0 2.2 %copy-start.1 = (bf16[16,18432]{1,0:T(8,128)(2,1)S(1)}, bf16[16,18432]{1,0:T(8,128)(2,1)}, u32[]{:S(2)}) copy-start(bf16[16,18432]{1,0:T(8,128)(2,1)} %slice.240) | copy-start | bytes 1769476
  85.8 2.8 %copy-start.14 = (bf16[8,192]{1,0:T(8,128)(2,1)S(1)}, bf16[8,192]{1,0:T(8,128)(2,1)}, u32[]{:S(2)}) copy-start(bf16[8,192]{1,0:T(8,128)(2,1)} %param.12) | copy-start | bytes 9220
  85.8 3.0 %copy-start.8 = (bf16[8,8,256]{2,0,1:T(8,128)(2,1)S(1)}, bf16[8,8,256]{2,0,1:T(8,128)(2,1)}, u32[]{:S(2)}) copy-start(bf16[8,8,256]{2,0,1:T(8,128)(2,1)} %copy-done.7) | copy-start | bytes 98308
  85.8 3.0 %copy-start.10 = (bf16[8,8,256]{2,0,1:T(8,128)(2,1)S(1)}, bf16[8,8,256]{2,0,1:T(8,128)(2,1)}, u32[]{:S(2)}) copy-start(bf16[8,8,256]{2,0,1:T(8,128)(2,1)} %copy-done.9) | copy-start | bytes 98308
  85.8 3.0 %copy-start.13 = (s32[6]{0:T(128)S(1)}, s32[6]{0:T(128)}, u32[]{:S(2)}) copy-start(s32[6]{0:T(128)} %copy-done.12) | copy-start | bytes 76

commit v6 on v5

--- a/solution.py
+++ b/solution.py
@@ -125,7 +125,7 @@
     total = None
     for piece, spots in pieces:
         term = jnp.einsum(
-            "cbq,qp->cbp", piece, place_matrix(spots, width), preferred_element_type=jnp.float32
+            "cbq,qp->bcp", piece, place_matrix(spots, width), preferred_element_type=jnp.float32
         )
         total = term if total is None else total + term
     return total.astype(jnp.bfloat16)
@@ -134,13 +134,22 @@
 def conv_cm(weight, padded):
     row_width = SIDE + 2
     out_span = SIDE * row_width
-    products = jnp.einsum("toc,cbp->tobp", weight, padded, preferred_element_type=jnp.float32)
+    taps, out_chans, in_chans = weight.shape
+    rows = -(-out_chans // 8) * 8
+    weight = jnp.pad(weight, ((0, 0), (0, rows - out_chans), (0, 0)))
+    tile_count = padded.shape[0]
+    products = jnp.einsum(
+        "kc,bcp->bkp",
+        weight.reshape(taps * rows, in_chans),
+        padded,
+        preferred_element_type=jnp.float32,
+    ).reshape(tile_count, taps, rows, padded.shape[2])
     accum = None
-    for tap_index in range(weight.shape[0]):
+    for tap_index in range(taps):
         offset = tap_index // 3 * row_width + tap_index % 3
-        term = products[tap_index, :, :, offset : offset + out_span]
+        term = products[:, tap_index, :out_chans, offset : offset + out_span]
         accum = term if accum is None else accum + term
-    return jnp.transpose(accum, (1, 0, 2))
+    return accum
 
 
 def pick(selector, values, spec):

time: 90.6 us -> 88.1 us (0.972)
  other arithmetic: 5.82 us -> 2.95 us
  local copies, waits for them, and re-layouts: 14.1 us -> 15.5 us
    transpose x1 -> x0, other arithmetic: 2 us -> none  [conv_cm(): return jnp.transpose(accum, (1, 0, 2))]
    slice x0 -> x1, local copies, waits for them, and re-layouts: none -> 1.99 us  [conv_cm(): term = products[:, tap_index, :out_chans, offset:offset + out_span]]
    unnamed x38 -> x31, local copies, waits for them, and re-layouts: 4.69 us -> 4.68 us
  transfers between devices with their start and end apart: 3 -> 3, of which waited for: 2 -> 2; matrix products, arithmetic and copies ran while one was open for 5% -> 6% of each run, Pallas kernels for 0% -> 0%
where the time goes in v6:
time: 88.1 us; the launch traced here: 87.2 us
  blocking collectives  47.9 us (54%)
  local copies, waits for them, and re-layouts  15.5 us (18%)
  starting transfers between devices  10.9 us (12%)
  matrix products  7.76 us (9%)
  other arithmetic  2.95 us (3%)
  between operations  1.32 us (1%)
  waiting for transfers between devices  0.92 us (1%)
    all_gather x2, blocking collectives, gather_rows(): gathered = lax.all_gather(rows, 'chan', axis=0, tiled=False)  47.9 us
    ppermute x1, starting transfers between devices, local(): lax.ppermute(outgoing, 'tiles', [((i + 1) % groups, i) for i in range(gro...  8.95 us
    unnamed x31, local copies, waits for them, and re-layouts  4.68 us
    dot_general x2, matrix products, conv_cm(): jnp.einsum('kc,bcp->bkp', weight.reshape(taps * rows, in_chans), padded,...  3.94 us
    reshape x6, local copies, waits for them, and re-layouts, gather_rows(): parts.append(part.reshape((groups * piece.shape[0],) + piece.shape[1:]))  3.58 us
    dot_general x7, matrix products, pick(): jnp.einsum(spec, selector, values, preferred_element_type=jnp.float32)  2.25 us
    slice x1, local copies, waits for them, and re-layouts, conv_cm(): term = products[:, tap_index, :out_chans, offset:offset + out_span]  1.99 us
    ppermute x1, starting transfers between devices, partner(): return lax.ppermute(value, axis, pairs)  1.92 us
  transfers between devices with their start and end apart: 3, of which 2 were waited for; matrix products, arithmetic and copies ran while one was open for 6% of the time, Pallas kernels for 0%

profile of v6, /device:TPU:6, one launch (start us, length us, event | category | flops | bytes accessed | tf_op | source)
XLA Modules:
  0.0 87.2 jit_solution(986502124429434756)
XLA Ops:
  0.7 0.8 fusion.77
  1.5 0.8 copy.263
  2.3 0.8 copy.198
  3.2 1.0 %fusion.10 = bf16[20,8,64]{2,0,1:T(8,128)(2,1)S(1)} fusion(bf16[8,8,256]{2,1,0:T(8,128)(2,1)} %param.9, bf16[8,12,256]{2,1,0:T(8,128)(2,1)S(1)} %copy.198, s32[64]{0:T(128)S(1)} %get-tuple-element.29), kind=kOutput, calls=%fused_computation.20 | convolution fusion | flops 5433344 | bytes 102656 | tf_op jit(solution)/shard_map/qe,bcq->cbe/dot_general | solution.py:156
  4.5 8.9 %collective-permute-start.1 = (bf16[26624]{0:T(1024)(128)(2,1)S(1)}, bf16[26624]{0:T(1024)(128)(2,1)S(1)}, u32[]{:S(2)}, u32[]{:S(2)}) collective-permute-start(bf16[26624]{0:T(1024)(128)(2,1)S(1)} %constant_dynamic-update-slice_fusion), channel_id=1, source_target_pairs={{16,0},{32,16},{48,32},{64,48},{80,64},{96,80},{112,96},{128,112},... | collective-permute-start | bytes 159752 | tf_op jit(solution)/shard_map/ppermute | solution.py:208
  13.5 0.8 dynamic_slice.7
  15.1 0.5 fusion.107
  15.8 0.8 copy.262
  16.8 0.9 %pad.4 = bf16[9,16,192]{2,1,0:T(8,128)(2,1)S(1)} pad(bf16[9,12,192]{2,1,0:T(8,128)(2,1)} %param.10, bf16[]{:T(256)} %constant.177.clone.1), padding=0_0x0_4x0_0 | pad | bytes 96770 | tf_op jit(solution)/shard_map/jit(_pad)/pad | solution.py:139
  20.2 24.7 %all_gather.6 = bf16[16,126,256]{2,1,0:T(8,128)(2,1)S(1)} all-gather(bf16[1,126,256]{2,1,0:T(8,128)(2,1)S(1)} %all_gather_reshape.6), channel_id=1, replica_groups=mesh['tiles'=32,'chan'=16] {'chan'}, dimensions={0}, use_global_device_ids=true | all-gather | bytes 1096704 | tf_op jit(solution)/shard_map/all_gather | solution.py:94
  45.0 0.6 copy.264
  46.3 1.2 %reshape.296 = bf16[192,8,64]{2,1,0:T(8,128)(2,1)} reshape(bf16[16,6144]{1,0:T(8,128)(2,1)S(1)} %slice.214) | data formatting | bytes 393216 | tf_op jit(solution)/shard_map/reshape | solution.py:102
  47.7 0.6 fusion.13
  48.3 3.2 %fusion.1 = f32[8,326,144]{1,2,0:T(8,128)} fusion(bf16[144,192,1]{1,0,2:T(8,128)(2,1)S(1)} %bitcast.174, f32[326,192,8]{0,1,2:T(8,128)S(1)} %fusion.13, bf16[192,8,64]{2,1,0:T(8,128)(2,1)} %reshape.296, s32[64]{0:T(128)S(1)} %get-tuple-element.30), kind=kOutput, calls=%fused_computation.2 | convolution fusion | flops 209328512 | bytes 3757312 | tf_op jit(solution)/shard_map/kc,bcp->bkp/dot_general | solution.py:141
  51.5 2.0 %fusion.114 = (f32[8,1,12,288]{3,2,1,0:T(8,128)S(1)}, f32[8,1,12,288]{3,2,1,0:T(8,128)S(1)}, f32[8,1,12,288]{3,2,1,0:T(8,128)S(1)}, f32[8,1,12,288]{3,2,1,0:T(8,...) fusion(f32[8,9,16,326]{3,2,1,0:T(8,128)} %bitcast.159), kind=kLoop, calls=%fused_computation.200 | loop fusion | bytes 1990656 | tf_op jit(solution)/shard_map/slice | solution.py:150
  53.9 0.5 reshape.321
  54.8 1.9 %collective-permute-start.2 = (bf16[8,3584]{1,0:T(8,128)(2,1)S(1)}, bf16[8,3584]{1,0:T(8,128)(2,1)S(1)}, u32[]{:S(2)}, u32[]{:S(2)}) collective-permute-start(bf16[8,3584]{1,0:T(8,128)(2,1)S(1)} %pad_maximum_fusion.5), channel_id=1, source_target_pairs={{0,16},{16,0},{32,48},{48,32},{64,80},{80,64},{96,112},{112,96},{1... | collective-permute-start | bytes 172040 | tf_op jit(solution)/shard_map/ppermute | solution.py:28
  57.4 0.6 collective-permute-done.2
  58.7 23.1 %all_gather.7 = bf16[16,126,256]{2,1,0:T(8,128)(2,1)S(1)} all-gather(bf16[1,126,256]{2,1,0:T(8,128)(2,1)S(1)} %all_gather_reshape.7), channel_id=1, replica_groups=mesh['tiles'=32,'chan'=16] {'chan'}, dimensions={0}, use_global_device_ids=true | all-gather | bytes 1096704 | tf_op jit(solution)/shard_map/all_gather | solution.py:94
  81.8 0.6 copy.265
  82.7 0.8 reshape.309
  83.9 0.7 convolution_bitcast_fusion
  84.8 0.9 %reshape.314 = bf16[192,6,256]{2,1,0:T(8,128)(2,1)S(1)} reshape(bf16[16,18432]{1,0:T(8,128)(2,1)S(1)} %slice.240) | data formatting | bytes 1179648 | tf_op jit(solution)/shard_map/reshape | solution.py:102
  86.6 0.6 copy.241
  (119 shorter events, 8.6 us)
Async XLA Ops:
  0.6 83.2 %copy-start = (bf16[9,8,128]{2,1,0:T(8,128)(2,1)S(1)}, bf16[9,8,128]{2,1,0:T(8,128)(2,1)}, u32[]{:S(2)}) copy-start(bf16[9,8,128]{2,1,0:T(8,128)(2,1)} %param.11) | copy-start | bytes 55300
  0.6 18.5 %copy-start.3 = (bf16[8,8,256]{2,1,0:T(8,128)(2,1)S(1)}, bf16[8,8,256]{2,1,0:T(8,128)(2,1)}, u32[]{:S(2)}) copy-start(bf16[8,8,256]{2,1,0:T(8,128)(2,1)} %param.9) | copy-start | bytes 98308
  4.5 13.2 %collective-permute-start.1 = (bf16[26624]{0:T(1024)(128)(2,1)S(1)}, bf16[26624]{0:T(1024)(128)(2,1)S(1)}, u32[]{:S(2)}, u32[]{:S(2)}) collective-permute-start(bf16[26624]{0:T(1024)(128)(2,1)S(1)} %constant_dynamic-update-slice_fusion), channel_id=1, source_target_pairs={{16,0},{32,16},{48,32},{64,48},{80,64},{96,80},{112,96},{128,112},... | collective-permute-start | bytes 159752 | tf_op jit(solution)/shard_map/ppermute | solution.py:208
  13.4 4.8 %collective-permute-start = (bf16[26624]{0:T(1024)(128)(2,1)S(1)}, bf16[26624]{0:T(1024)(128)(2,1)S(1)}, u32[]{:S(2)}, u32[]{:S(2)}) collective-permute-start(bf16[26624]{0:T(1024)(128)(2,1)S(1)} %constant_dynamic-update-slice_fusion), channel_id=1, source_target_pairs={{0,16},{16,32},{32,48},{48,64},{64,80},{80,96},{96,112},{112,128},... | collective-permute-start | bytes 159752 | tf_op jit(solution)/shard_map/ppermute | solution.py:207
  14.9 4.5 %copy-start.8 = (s32[6]{0:T(128)}, s32[6]{0:T(128)S(1)}, u32[]{:S(2)}) copy-start(s32[6]{0:T(128)S(1)} %convert_reduce_fusion) | copy-start | bytes 76
  19.2 0.6 copy-start.4
  19.2 26.3 %copy-start.6 = (bf16[8,8,256]{2,0,1:T(8,128)(2,1)}, bf16[8,8,256]{2,0,1:T(8,128)(2,1)S(1)}, u32[]{:S(2)}) copy-start(bf16[8,8,256]{2,0,1:T(8,128)(2,1)S(1)} %get-tuple-element.26) | copy-start | bytes 98308
  53.5 1.2 %copy-start.1 = (bf16[8,12,256]{2,0,1:T(8,128)(2,1)S(1)}, bf16[8,12,256]{2,0,1:T(8,128)(2,1)}, u32[]{:S(2)}) copy-start(bf16[8,12,256]{2,0,1:T(8,128)(2,1)} %param.8) | copy-start | bytes 147460
  53.5 3.2 %copy-start.10 = (s32[32]{0:T(128)S(1)}, s32[32]{0:T(128)}, u32[]{:S(2)}) copy-start(s32[32]{0:T(128)} %fusion.107) | copy-start | bytes 388
  53.9 4.1 %copy-start.9 = (s32[6]{0:T(128)S(1)}, s32[6]{0:T(128)}, u32[]{:S(2)}) copy-start(s32[6]{0:T(128)} %copy-done.8) | copy-start | bytes 76
  54.8 27.6 %copy-start.2 = (bf16[8,12,256]{2,0,1:T(8,128)(2,1)}, bf16[8,12,256]{2,0,1:T(8,128)(2,1)S(1)}, u32[]{:S(2)}) copy-start(bf16[8,12,256]{2,0,1:T(8,128)(2,1)S(1)} %fusion.38) | copy-start | bytes 147460
  54.8 3.1 %collective-permute-start.2 = (bf16[8,3584]{1,0:T(8,128)(2,1)S(1)}, bf16[8,3584]{1,0:T(8,128)(2,1)S(1)}, u32[]{:S(2)}, u32[]{:S(2)}) collective-permute-start(bf16[8,3584]{1,0:T(8,128)(2,1)S(1)} %pad_maximum_fusion.5), channel_id=1, source_target_pairs={{0,16},{16,0},{32,48},{48,32},{64,80},{80,64},{96,112},{112,96},{1... | collective-permute-start | bytes 172040 | tf_op jit(solution)/shard_map/ppermute | solution.py:28
  83.8 2.3 %copy-start.11 = (bf16[8,192]{1,0:T(8,128)(2,1)S(1)}, bf16[8,192]{1,0:T(8,128)(2,1)}, u32[]{:S(2)}) copy-start(bf16[8,192]{1,0:T(8,128)(2,1)} %param.12) | copy-start | bytes 9220
  83.8 2.5 %copy-start.5 = (bf16[8,8,256]{2,0,1:T(8,128)(2,1)S(1)}, bf16[8,8,256]{2,0,1:T(8,128)(2,1)}, u32[]{:S(2)}) copy-start(bf16[8,8,256]{2,0,1:T(8,128)(2,1)} %copy-done.4) | copy-start | bytes 98308
  83.9 2.5 %copy-start.7 = (bf16[8,8,256]{2,0,1:T(8,128)(2,1)S(1)}, bf16[8,8,256]{2,0,1:T(8,128)(2,1)}, u32[]{:S(2)}) copy-start(bf16[8,8,256]{2,0,1:T(8,128)(2,1)} %copy-done.6) | copy-start | bytes 98308

commit v7 on v6

--- a/solution.py
+++ b/solution.py
@@ -192,18 +192,22 @@
     per_owner = per_dev * 3 // 4
     parity = tile_group % 2
 
-    both_states = jnp.concatenate([atmos_state, ocean_state], axis=1)
-    edges_cm = pick(edge_matrix(), both_states, "qe,bcq->cbe")
     tables = lax.dynamic_slice_in_dim(
         jnp.concatenate([neighbours, rotations, sea_mask[:, None]], axis=1), first_tile, per_dev, 0
     )
     sea_here = tables[:, 8].astype(jnp.bfloat16)
+    edge_pick = edge_matrix()
     edges_cm = jnp.concatenate(
-        [edges_cm[:atmos_local], edges_cm[atmos_local:] * sea_here[None, :, None]], axis=0
-    )
-    edge_flat = edges_cm.reshape(-1)
-    edge_size = edge_flat.shape[0]
-    outgoing = jnp.concatenate([edge_flat, ocean_state.reshape(-1)])
+        [
+            pick(edge_pick, atmos_state, "qe,bcq->cbe"),
+            pick(edge_pick, ocean_state, "qe,bcq->cbe") * sea_here[None, :, None],
+        ],
+        axis=0,
+    )
+    edge_rows = edges_cm.size // pixels
+    outgoing = jnp.concatenate(
+        [edges_cm.reshape(edge_rows, pixels), ocean_state.reshape(-1, pixels)], axis=0
+    )
     from_left = lax.ppermute(outgoing, "tiles", [(i, (i + 1) % groups) for i in range(groups)])
     from_right = lax.ppermute(outgoing, "tiles", [((i + 1) % groups, i) for i in range(groups)])
 
@@ -236,16 +240,16 @@
         == SIDE - 1 - lax.broadcasted_iota(jnp.int32, (SIDE, SIDE), 1)
     ).astype(jnp.bfloat16)
 
-    partner_state = jnp.where(parity == 0, from_right[edge_size:], from_left[edge_size:])
+    partner_state = jnp.where(parity == 0, from_right[edge_rows:], from_left[edge_rows:])
     pair_state = pair_order(ocean_state, partner_state.reshape(ocean_state.shape), parity)
     ocean_cm = pick(own_pick, pair_state, "st,tcp->csp")
     own_ocean = pick(own_pick, pair_state, "st,tcp->scp")
 
     widened = jnp.concatenate(
         [
-            from_left[:edge_size].reshape(edges_cm.shape),
+            from_left[:edge_rows].reshape(edges_cm.shape),
             edges_cm,
-            from_right[:edge_size].reshape(edges_cm.shape),
+            from_right[:edge_rows].reshape(edges_cm.shape),
         ],
         axis=1,
     ).reshape(chans, 3 * per_dev * 4, SIDE)

time: 88.1 us -> 87.8 us (level)
  local copies, waits for them, and re-layouts: 15.5 us -> 13.5 us
  matrix products: 7.76 us -> 8.75 us
    unnamed x31 -> x28, local copies, waits for them, and re-layouts: 4.68 us -> 2.69 us
    dot_general x7 -> x8, matrix products: 2.25 us -> 3.23 us  [pick(): jnp.einsum(spec, selector, values, preferred_element_type=jnp.float32)]
where the time goes in v7:
time: 87.8 us; the launch traced here: 86.8 us
  blocking collectives  47.9 us (55%)
  local copies, waits for them, and re-layouts  13.5 us (15%)
  starting transfers between devices  10.9 us (12%)
  matrix products  8.75 us (10%)
  other arithmetic  3.65 us (4%)
  between operations  1.3 us (1%)
  waiting for transfers between devices  0.91 us (1%)
    all_gather x2, blocking collectives, gather_rows(): gathered = lax.all_gather(rows, 'chan', axis=0, tiled=False)  47.9 us
    ppermute x1, starting transfers between devices, local(): lax.ppermute(outgoing, 'tiles', [((i + 1) % groups, i) for i in range(gro...  8.93 us
    dot_general x2, matrix products, conv_cm(): jnp.einsum('kc,bcp->bkp', weight.reshape(taps * rows, in_chans), padded,...  3.94 us
    reshape x6, local copies, waits for them, and re-layouts, gather_rows(): parts.append(part.reshape((groups * piece.shape[0],) + piece.shape[1:]))  3.58 us
    dot_general x8, matrix products, pick(): jnp.einsum(spec, selector, values, preferred_element_type=jnp.float32)  3.23 us
    unnamed x28, local copies, waits for them, and re-layouts  2.69 us
    slice x1, local copies, waits for them, and re-layouts, conv_cm(): term = products[:, tap_index, :out_chans, offset:offset + out_span]  1.99 us
    ppermute x1, starting transfers between devices, partner(): return lax.ppermute(value, axis, pairs)  1.92 us
  transfers between devices with their start and end apart: 3, of which 2 were waited for; matrix products, arithmetic and copies ran while one was open for 6% of the time, Pallas kernels for 0%

profile of v7, /device:TPU:6, one launch (start us, length us, event | category | flops | bytes accessed | tf_op | source)
XLA Modules:
  0.0 86.8 jit_solution(13907656935992508192)
XLA Ops:
  0.7 0.8 fusion.80
  1.6 1.0 %fusion.11 = bf16[12,8,64]{2,0,1:T(8,128)(2,1)S(1)} fusion(bf16[8,12,256]{2,0,1:T(8,128)(2,1)} %param.8, s32[64]{0:T(128)S(1)} %get-tuple-element.29), kind=kOutput, calls=%fused_computation.21 | convolution fusion | flops 3168256 | bytes 61696 | tf_op jit(solution)/shard_map/qe,bcq->cbe/dot_general | solution.py:156
  2.6 1.0 %fusion.14 = bf16[8,8,64]{2,0,1:T(8,128)(2,1)S(1)} fusion(bf16[8,8,256]{2,1,0:T(8,128)(2,1)} %param.9, s32[64]{0:T(128)S(1)} %get-tuple-element.29, bf16[8]{0:T(256)(128)(2,1)S(1)} %fusion.113), kind=kOutput, calls=%fused_computation.26 | convolution fusion | flops 2121728 | bytes 41232 | tf_op jit(solution)/shard_map/qe,bcq->cbe/dot_general | solution.py:156
  3.8 0.8 pad_maximum_fusion.6
  4.5 8.9 %collective-permute-start.1 = (bf16[104,256]{1,0:T(8,128)(2,1)S(1)}, bf16[104,256]{1,0:T(8,128)(2,1)S(1)}, u32[]{:S(2)}, u32[]{:S(2)}) collective-permute-start(bf16[104,256]{1,0:T(8,128)(2,1)S(1)} %pad_maximum_fusion.6), channel_id=1, source_target_pairs={{16,0},{32,16},{48,32},{64,48},{80,64},{96,80},{112,96},{128,112},... | collective-permute-start | bytes 159752 | tf_op jit(solution)/shard_map/ppermute | solution.py:212
  13.5 0.8 dynamic_slice.7
  15.1 0.5 fusion.110
  15.8 0.8 copy.262
  16.8 0.9 %pad.4 = bf16[9,16,192]{2,1,0:T(8,128)(2,1)S(1)} pad(bf16[9,12,192]{2,1,0:T(8,128)(2,1)} %param.10, bf16[]{:T(256)} %constant.177.clone.1), padding=0_0x0_4x0_0 | pad | bytes 96770 | tf_op jit(solution)/shard_map/jit(_pad)/pad | solution.py:139
  19.8 24.7 %all_gather.6 = bf16[16,126,256]{2,1,0:T(8,128)(2,1)S(1)} all-gather(bf16[1,126,256]{2,1,0:T(8,128)(2,1)S(1)} %all_gather_reshape.6), channel_id=1, replica_groups=mesh['tiles'=32,'chan'=16] {'chan'}, dimensions={0}, use_global_device_ids=true | all-gather | bytes 1096704 | tf_op jit(solution)/shard_map/all_gather | solution.py:94
  44.6 0.6 copy.263
  46.0 1.2 %reshape.265 = bf16[192,8,64]{2,1,0:T(8,128)(2,1)} reshape(bf16[16,6144]{1,0:T(8,128)(2,1)S(1)} %slice.172) | data formatting | bytes 393216 | tf_op jit(solution)/shard_map/reshape | solution.py:102
  47.3 0.6 fusion.15
  47.9 3.2 %fusion.1 = f32[8,326,144]{1,2,0:T(8,128)} fusion(bf16[144,192,1]{1,0,2:T(8,128)(2,1)S(1)} %bitcast.178, f32[326,192,8]{0,1,2:T(8,128)S(1)} %fusion.15, bf16[192,8,64]{2,1,0:T(8,128)(2,1)} %reshape.265, s32[64]{0:T(128)S(1)} %get-tuple-element.30), kind=kOutput, calls=%fused_computation.2 | convolution fusion | flops 209328512 | bytes 3757312 | tf_op jit(solution)/shard_map/kc,bcp->bkp/dot_general | solution.py:141
  51.2 2.0 %fusion.116 = (f32[8,1,12,288]{3,2,1,0:T(8,128)S(1)}, f32[8,1,12,288]{3,2,1,0:T(8,128)S(1)}, f32[8,1,12,288]{3,2,1,0:T(8,128)S(1)}, f32[8,1,12,288]{3,2,1,0:T(8,...) fusion(f32[8,9,16,326]{3,2,1,0:T(8,128)} %bitcast.164), kind=kLoop, calls=%fused_computation.200 | loop fusion | bytes 1990656 | tf_op jit(solution)/shard_map/slice | solution.py:150
  53.5 0.5 reshape.290
  54.5 1.9 %collective-permute-start.2 = (bf16[8,3584]{1,0:T(8,128)(2,1)S(1)}, bf16[8,3584]{1,0:T(8,128)(2,1)S(1)}, u32[]{:S(2)}, u32[]{:S(2)}) collective-permute-start(bf16[8,3584]{1,0:T(8,128)(2,1)S(1)} %pad_maximum_fusion.5), channel_id=1, source_target_pairs={{0,16},{16,0},{32,48},{48,32},{64,80},{80,64},{96,112},{112,96},{1... | collective-permute-start | bytes 172040 | tf_op jit(solution)/shard_map/ppermute | solution.py:28
  57.0 0.6 collective-permute-done.2
  58.3 23.1 %all_gather.7 = bf16[16,126,256]{2,1,0:T(8,128)(2,1)S(1)} all-gather(bf16[1,126,256]{2,1,0:T(8,128)(2,1)S(1)} %all_gather_reshape.7), channel_id=1, replica_groups=mesh['tiles'=32,'chan'=16] {'chan'}, dimensions={0}, use_global_device_ids=true | all-gather | bytes 1096704 | tf_op jit(solution)/shard_map/all_gather | solution.py:94
  81.4 0.6 copy.264
  82.3 0.8 reshape.278
  83.5 0.7 convolution_bitcast_fusion
  84.5 0.9 %reshape.283 = bf16[192,6,256]{2,1,0:T(8,128)(2,1)S(1)} reshape(bf16[16,18432]{1,0:T(8,128)(2,1)S(1)} %slice.198) | data formatting | bytes 1179648 | tf_op jit(solution)/shard_map/reshape | solution.py:102
  86.2 0.6 copy.241
  (114 shorter events, 8.1 us)
Async XLA Ops:
  0.6 82.8 %copy-start = (bf16[9,8,128]{2,1,0:T(8,128)(2,1)S(1)}, bf16[9,8,128]{2,1,0:T(8,128)(2,1)}, u32[]{:S(2)}) copy-start(bf16[9,8,128]{2,1,0:T(8,128)(2,1)} %param.11) | copy-start | bytes 55300
  0.6 18.6 %copy-start.3 = (bf16[8,8,256]{2,1,0:T(8,128)(2,1)S(1)}, bf16[8,8,256]{2,1,0:T(8,128)(2,1)}, u32[]{:S(2)}) copy-start(bf16[8,8,256]{2,1,0:T(8,128)(2,1)} %param.9) | copy-start | bytes 98308
  4.5 13.2 %collective-permute-start.1 = (bf16[104,256]{1,0:T(8,128)(2,1)S(1)}, bf16[104,256]{1,0:T(8,128)(2,1)S(1)}, u32[]{:S(2)}, u32[]{:S(2)}) collective-permute-start(bf16[104,256]{1,0:T(8,128)(2,1)S(1)} %pad_maximum_fusion.6), channel_id=1, source_target_pairs={{16,0},{32,16},{48,32},{64,48},{80,64},{96,80},{112,96},{128,112},... | collective-permute-start | bytes 159752 | tf_op jit(solution)/shard_map/ppermute | solution.py:212
  13.5 4.8 %collective-permute-start = (bf16[104,256]{1,0:T(8,128)(2,1)S(1)}, bf16[104,256]{1,0:T(8,128)(2,1)S(1)}, u32[]{:S(2)}, u32[]{:S(2)}) collective-permute-start(bf16[104,256]{1,0:T(8,128)(2,1)S(1)} %pad_maximum_fusion.6), channel_id=1, source_target_pairs={{0,16},{16,32},{32,48},{48,64},{64,80},{80,96},{96,112},{112,128},... | collective-permute-start | bytes 159752 | tf_op jit(solution)/shard_map/ppermute | solution.py:211
  14.9 4.5 %copy-start.8 = (s32[6]{0:T(128)}, s32[6]{0:T(128)S(1)}, u32[]{:S(2)}) copy-start(s32[6]{0:T(128)S(1)} %convert_reduce_fusion) | copy-start | bytes 76
  19.2 25.9 %copy-start.6 = (bf16[8,8,256]{2,0,1:T(8,128)(2,1)}, bf16[8,8,256]{2,0,1:T(8,128)(2,1)S(1)}, u32[]{:S(2)}) copy-start(bf16[8,8,256]{2,0,1:T(8,128)(2,1)S(1)} %get-tuple-element.26) | copy-start | bytes 98308
  19.2 26.0 %copy-start.4 = (bf16[8,8,256]{2,0,1:T(8,128)(2,1)}, bf16[8,8,256]{2,0,1:T(8,128)(2,1)S(1)}, u32[]{:S(2)}) copy-start(bf16[8,8,256]{2,0,1:T(8,128)(2,1)S(1)} %get-tuple-element.25) | copy-start | bytes 98308
  53.1 1.2 %copy-start.2 = (bf16[8,12,256]{2,0,1:T(8,128)(2,1)S(1)}, bf16[8,12,256]{2,0,1:T(8,128)(2,1)}, u32[]{:S(2)}) copy-start(bf16[8,12,256]{2,0,1:T(8,128)(2,1)} %param.8) | copy-start | bytes 147460
  53.2 3.2 %copy-start.10 = (s32[32]{0:T(128)S(1)}, s32[32]{0:T(128)}, u32[]{:S(2)}) copy-start(s32[32]{0:T(128)} %fusion.110) | copy-start | bytes 388
  53.5 4.1 %copy-start.9 = (s32[6]{0:T(128)S(1)}, s32[6]{0:T(128)}, u32[]{:S(2)}) copy-start(s32[6]{0:T(128)} %copy-done.8) | copy-start | bytes 76
  54.4 27.6 %copy-start.1 = (bf16[8,12,256]{2,0,1:T(8,128)(2,1)}, bf16[8,12,256]{2,0,1:T(8,128)(2,1)S(1)}, u32[]{:S(2)}) copy-start(bf16[8,12,256]{2,0,1:T(8,128)(2,1)S(1)} %fusion.40) | copy-start | bytes 147460
  54.5 3.1 %collective-permute-start.2 = (bf16[8,3584]{1,0:T(8,128)(2,1)S(1)}, bf16[8,3584]{1,0:T(8,128)(2,1)S(1)}, u32[]{:S(2)}, u32[]{:S(2)}) collective-permute-start(bf16[8,3584]{1,0:T(8,128)(2,1)S(1)} %pad_maximum_fusion.5), channel_id=1, source_target_pairs={{0,16},{16,0},{32,48},{48,32},{64,80},{80,64},{96,112},{112,96},{1... | collective-permute-start | bytes 172040 | tf_op jit(solution)/shard_map/ppermute | solution.py:28
  83.5 2.3 %copy-start.11 = (bf16[8,192]{1,0:T(8,128)(2,1)S(1)}, bf16[8,192]{1,0:T(8,128)(2,1)}, u32[]{:S(2)}) copy-start(bf16[8,192]{1,0:T(8,128)(2,1)} %param.12) | copy-start | bytes 9220
  83.5 2.5 %copy-start.5 = (bf16[8,8,256]{2,0,1:T(8,128)(2,1)S(1)}, bf16[8,8,256]{2,0,1:T(8,128)(2,1)}, u32[]{:S(2)}) copy-start(bf16[8,8,256]{2,0,1:T(8,128)(2,1)} %copy-done.4) | copy-start | bytes 98308
  83.5 2.5 %copy-start.7 = (bf16[8,8,256]{2,0,1:T(8,128)(2,1)S(1)}, bf16[8,8,256]{2,0,1:T(8,128)(2,1)}, u32[]{:S(2)}) copy-start(bf16[8,8,256]{2,0,1:T(8,128)(2,1)} %copy-done.6) | copy-start | bytes 98308

commit v8 on v6

--- a/solution.py
+++ b/solution.py
@@ -277,8 +277,8 @@
         own_pick, pair_late[:, force_width:].reshape(2 * per_dev, ocean_local, 4 * SIDE), "st,tcp->csp"
     )
 
-    ocean_tail, ocean_rims, force_all = gather_rows(
-        [ocean_cm[:, :, early:], own_rims_cm, forcing_cm]
+    ocean_tail, ocean_rims, force_rows = gather_rows(
+        [ocean_cm[:, :, early:], own_rims_cm, forcing_cm.reshape(-1, pixels)]
     )
     ocean_pad = placed(
         [
@@ -288,9 +288,13 @@
         ]
     )
     conv_accum = conv_cm(ocean_weight, ocean_pad)
+    tile_eye = jnp.eye(per_owner, dtype=couple_weight.dtype)
+    couple_rows = (couple_weight[None, :, :, None] * tile_eye[:, None, None, :]).reshape(
+        per_owner * couple_weight.shape[0], -1
+    )
     couple_accum = jnp.einsum(
-        "oc,cbp->bop", couple_weight, force_all, preferred_element_type=jnp.float32
-    )
+        "kr,rp->kp", couple_rows, force_rows, preferred_element_type=jnp.float32
+    ).reshape(per_owner, couple_weight.shape[0], pixels)
     mixed = trim_columns(conv_accum) + couple_accum
     ocean_next = (own_ocean.astype(jnp.float32) + jax.nn.gelu(mixed, approximate=True)).astype(
         jnp.bfloat16

time: 88.1 us -> 91.2 us (1.035)
  other arithmetic: 2.95 us -> 4.76 us
  matrix products: 7.76 us -> 9.17 us
    mul x0 -> x4, local copies, waits for them, and re-layouts: none -> 1.87 us  [local(): couple_weight[None, :, :, None] * tile_eye[:, None, None, :]]
    add x3, other arithmetic: 0.53 us -> 1.73 us  [interior_spots(): return (pixel // SIDE + 1) * (SIDE + 2) + pixel % SIDE + 1]
    unnamed x31 -> x41, local copies, waits for them, and re-layouts: 4.68 us -> 4.01 us
  transfers between devices with their start and end apart: 3 -> 3, of which waited for: 2 -> 1; matrix products, arithmetic and copies ran while one was open for 6% -> 8% of each run, Pallas kernels for 0% -> 0%
where the time goes in v8:
time: 91.2 us; the launch traced here: 90.1 us
  blocking collectives  47.7 us (52%)
  local copies, waits for them, and re-layouts  15.8 us (17%)
  starting transfers between devices  10.9 us (12%)
  matrix products  9.17 us (10%)
  other arithmetic  4.76 us (5%)
  between operations  1.42 us (2%)
    all_gather x2, blocking collectives, gather_rows(): gathered = lax.all_gather(rows, 'chan', axis=0, tiled=False)  47.7 us
    ppermute x1, starting transfers between devices, local(): lax.ppermute(outgoing, 'tiles', [((i + 1) % groups, i) for i in range(gro...  8.95 us
    dot_general x2, matrix products, conv_cm(): jnp.einsum('kc,bcp->bkp', weight.reshape(taps * rows, in_chans), padded,...  4.62 us
    unnamed x41, local copies, waits for them, and re-layouts  4.01 us
    reshape x6, local copies, waits for them, and re-layouts, gather_rows(): parts.append(part.reshape((groups * piece.shape[0],) + piece.shape[1:]))  2.93 us
    dot_general x7, matrix products, pick(): jnp.einsum(spec, selector, values, preferred_element_type=jnp.float32)  2.25 us
    dot_general x3, matrix products, placed(): jnp.einsum('cbq,qp->bcp', piece, place_matrix(spots, width), preferred_el...  2.03 us
    slice x1, local copies, waits for them, and re-layouts, conv_cm(): term = products[:, tap_index, :out_chans, offset:offset + out_span]  1.99 us
  transfers between devices with their start and end apart: 3, of which 1 were waited for; matrix products, arithmetic and copies ran while one was open for 8% of the time, Pallas kernels for 0%

profile of v8, /device:TPU:6, one launch (start us, length us, event | category | flops | bytes accessed | tf_op | source)
XLA Modules:
  0.0 90.1 jit_solution(15828980396705312161)
XLA Ops:
  0.8 0.8 fusion.78
  1.5 0.8 copy.194
  2.4 0.7 pad_add_fusion
  3.0 1.0 %fusion.10 = bf16[20,8,64]{2,0,1:T(8,128)(2,1)S(1)} fusion(bf16[8,8,256]{2,1,0:T(8,128)(2,1)} %param.9, bf16[8,12,256]{2,1,0:T(8,128)(2,1)S(1)} %copy.194, s32[64]{0:T(128)S(1)} %get-tuple-element.29), kind=kOutput, calls=%fused_computation.21 | convolution fusion | flops 5433344 | bytes 102656 | tf_op jit(solution)/shard_map/qe,bcq->cbe/dot_general | solution.py:156
  4.3 0.8 copy.260
  5.1 8.9 %collective-permute-start.1 = (bf16[26624]{0:T(1024)(128)(2,1)S(1)}, bf16[26624]{0:T(1024)(128)(2,1)S(1)}, u32[]{:S(2)}, u32[]{:S(2)}) collective-permute-start(bf16[26624]{0:T(1024)(128)(2,1)S(1)} %constant_dynamic-update-slice_fusion), channel_id=1, source_target_pairs={{16,0},{32,16},{48,32},{64,48},{80,64},{96,80},{112,96},{128,112},... | collective-permute-start | bytes 159752 | tf_op jit(solution)/shard_map/ppermute | solution.py:208
  14.7 0.6 fusion.106
  15.2 0.8 dynamic_slice.7
  16.5 1.0 %mul.157 = bf16[8,192,6]{2,1,0:T(8,128)(2,1)S(1)} broadcast(bf16[8,192]{1,0:T(8,128)(2,1)} %param.12), dimensions={0,1} | broadcast | bytes 21504 | tf_op jit(solution)/shard_map/mul | solution.py:292
  18.7 0.6 fusion.108
  19.8 0.7 pad.4
  22.7 24.6 %all_gather.6 = bf16[16,126,256]{2,1,0:T(8,128)(2,1)S(1)} all-gather(bf16[1,126,256]{2,1,0:T(8,128)(2,1)S(1)} %all_gather_reshape.6), channel_id=1, replica_groups=mesh['tiles'=32,'chan'=16] {'chan'}, dimensions={0}, use_global_device_ids=true | all-gather | bytes 1096704 | tf_op jit(solution)/shard_map/all_gather | solution.py:94
  47.2 0.6 copy.261
  48.3 1.1 %reshape.314 = bf16[192,8,64]{2,1,0:T(8,128)(2,1)} reshape(bf16[16,6144]{1,0:T(8,128)(2,1)S(1)} %slice.214) | data formatting | bytes 393216 | tf_op jit(solution)/shard_map/reshape | solution.py:102
  49.5 0.6 fusion.13
  50.1 3.2 %fusion.1 = f32[8,326,144]{1,2,0:T(8,128)} fusion(bf16[144,192,1]{1,0,2:T(8,128)(2,1)S(1)} %bitcast.168, f32[326,192,8]{0,1,2:T(8,128)S(1)} %fusion.13, bf16[192,8,64]{2,1,0:T(8,128)(2,1)} %reshape.314, s32[64]{0:T(128)S(1)} %copy-done.11), kind=kOutput, calls=%fused_computation.2 | convolution fusion | flops 209328512 | bytes 3757312 | tf_op jit(solution)/shard_map/kc,bcp->bkp/dot_general | solution.py:141
  53.3 2.0 %fusion.115 = (f32[8,1,12,288]{3,2,1,0:T(8,128)S(1)}, f32[8,1,12,288]{3,2,1,0:T(8,128)S(1)}, f32[8,1,12,288]{3,2,1,0:T(8,128)S(1)}, f32[8,1,12,288]{3,2,1,0:T(8,...) fusion(f32[8,9,16,326]{3,2,1,0:T(8,128)} %bitcast.153), kind=kLoop, calls=%fused_computation.201 | loop fusion | bytes 1990656 | tf_op jit(solution)/shard_map/slice | solution.py:150
  56.9 1.9 %collective-permute-start.2 = (bf16[8,3584]{1,0:T(8,128)(2,1)S(1)}, bf16[8,3584]{1,0:T(8,128)(2,1)S(1)}, u32[]{:S(2)}, u32[]{:S(2)}) collective-permute-start(bf16[8,3584]{1,0:T(8,128)(2,1)S(1)} %pad_maximum_fusion.5), channel_id=1, source_target_pairs={{0,16},{16,0},{32,48},{48,32},{64,80},{80,64},{96,112},{112,96},{1... | collective-permute-start | bytes 172040 | tf_op jit(solution)/shard_map/ppermute | solution.py:28
  60.8 23.1 %all_gather.7 = bf16[16,126,256]{2,1,0:T(8,128)(2,1)S(1)} all-gather(bf16[1,126,256]{2,1,0:T(8,128)(2,1)S(1)} %all_gather_reshape.7), channel_id=1, replica_groups=mesh['tiles'=32,'chan'=16] {'chan'}, dimensions={0}, use_global_device_ids=true | all-gather | bytes 1096704 | tf_op jit(solution)/shard_map/all_gather | solution.py:94
  83.9 0.6 copy.262
  84.6 0.8 reshape.326
  85.6 1.0 %convolution_add_fusion = f32[326,128,6]{1,0,2:T(8,128)S(1)} fusion(f32[326,128,6]{1,0,2:T(8,128)S(1)} %fusion.24, bf16[128,6,224]{2,1,0:T(8,128)(2,1)S(1)} %reshape.326, s32[224]{0:T(256)} %fusion.106), kind=kOutput, calls=%fused_computation.3 | convolution fusion | flops 112488256 | bytes 2347904 | tf_op jit(solution)/shard_map/cbq,qp->bcp/dot_general | solution.py:127
  86.6 1.4 %convolution_bitcast_fusion = f32[6,9,8,326]{3,2,1,0:T(8,128)S(1)} fusion(f32[326,128,6]{1,0,2:T(8,128)S(1)} %convolution_add_fusion, bf16[128,6,64]{2,1,0:T(8,128)(2,1)S(1)} %reshape.327, s32[64]{0:T(128)} %get-tuple-element.30, bf16[9,8,128]{2,1,0:T(8,128)(2,1)S(1)} %copy-done), kind=kOutput, calls=%fused_computation.6 | convolution fusion | flops 68621696 | bytes 1681792 | tf_op jit(solution)/shard_map/kc,bcp->bkp/dot_general | solution.py:141
  89.5 0.6 copy.236
  (136 shorter events, 10.7 us)
Async XLA Ops:
  0.6 86.0 %copy-start = (bf16[9,8,128]{2,1,0:T(8,128)(2,1)S(1)}, bf16[9,8,128]{2,1,0:T(8,128)(2,1)}, u32[]{:S(2)}) copy-start(bf16[9,8,128]{2,1,0:T(8,128)(2,1)} %param.11) | copy-start | bytes 55300
  0.6 19.1 %copy-start.1 = (bf16[8,12,256]{2,0,1:T(8,128)(2,1)S(1)}, bf16[8,12,256]{2,0,1:T(8,128)(2,1)}, u32[]{:S(2)}) copy-start(bf16[8,12,256]{2,0,1:T(8,128)(2,1)} %param.8) | copy-start | bytes 147460
  0.7 19.8 %copy-start.7 = (bf16[8,8,256]{2,1,0:T(8,128)(2,1)S(1)}, bf16[8,8,256]{2,1,0:T(8,128)(2,1)}, u32[]{:S(2)}) copy-start(bf16[8,8,256]{2,1,0:T(8,128)(2,1)} %param.9) | copy-start | bytes 98308
  0.7 19.1 %copy-start.8 = (bf16[9,12,192]{2,1,0:T(8,128)(2,1)S(1)}, bf16[9,12,192]{2,1,0:T(8,128)(2,1)}, u32[]{:S(2)}) copy-start(bf16[9,12,192]{2,1,0:T(8,128)(2,1)} %param.10) | copy-start | bytes 124420
  5.1 15.3 %collective-permute-start = (bf16[26624]{0:T(1024)(128)(2,1)S(1)}, bf16[26624]{0:T(1024)(128)(2,1)S(1)}, u32[]{:S(2)}, u32[]{:S(2)}) collective-permute-start(bf16[26624]{0:T(1024)(128)(2,1)S(1)} %constant_dynamic-update-slice_fusion), channel_id=1, source_target_pairs={{0,16},{16,32},{32,48},{48,64},{64,80},{80,96},{96,112},{112,128},... | collective-permute-start | bytes 159752 | tf_op jit(solution)/shard_map/ppermute | solution.py:207
  5.1 15.3 %collective-permute-start.1 = (bf16[26624]{0:T(1024)(128)(2,1)S(1)}, bf16[26624]{0:T(1024)(128)(2,1)S(1)}, u32[]{:S(2)}, u32[]{:S(2)}) collective-permute-start(bf16[26624]{0:T(1024)(128)(2,1)S(1)} %constant_dynamic-update-slice_fusion), channel_id=1, source_target_pairs={{16,0},{32,16},{48,32},{64,48},{80,64},{96,80},{112,96},{128,112},... | collective-permute-start | bytes 159752 | tf_op jit(solution)/shard_map/ppermute | solution.py:208
  18.5 3.0 %copy-start.12 = (s32[6]{0:T(128)}, s32[6]{0:T(128)S(1)}, u32[]{:S(2)}) copy-start(s32[6]{0:T(128)S(1)} %convert_reduce_fusion) | copy-start | bytes 76
  20.5 0.8 copy-start.5
  20.7 0.6 copy-start.9
  22.4 25.6 %copy-start.4 = (bf16[20,32,16]{1,2,0:T(8,128)(2,1)}, bf16[20,32,16]{1,2,0:T(8,128)(2,1)S(1)}, u32[]{:S(2)}) copy-start(bf16[20,32,16]{1,2,0:T(8,128)(2,1)S(1)} %fusion.4) | copy-start | bytes 61444
  47.8 1.6 %copy-start.15 = (s32[256]{0:T(256)S(1)}, s32[256]{0:T(256)}, u32[]{:S(2)}) copy-start(s32[256]{0:T(256)} %fusion.102) | copy-start | bytes 3076
  48.0 2.1 %copy-start.3 = (bf16[9,16,192]{2,1,0:T(8,128)(2,1)S(1)}, bf16[9,16,192]{2,1,0:T(8,128)(2,1)}, u32[]{:S(2)}) copy-start(bf16[9,16,192]{2,1,0:T(8,128)(2,1)} %pad.4) | copy-start | bytes 165892
  48.0 2.1 %copy-start.11 = (s32[64]{0:T(128)S(1)}, s32[64]{0:T(128)}, u32[]{:S(2)}) copy-start(s32[64]{0:T(128)} %get-tuple-element.30) | copy-start | bytes 772
  55.3 1.3 %slice-start = ((bf16[20,32,16]{1,2,0:T(8,128)(2,1)}), bf16[8,32,16]{1,2,0:T(8,128)(2,1)S(1)}, s32[]{:S(2)}) async-start(bf16[20,32,16]{1,2,0:T(8,128)(2,1)} %copy-done.4), calls=%async_computation | async-start | bytes 65536 | tf_op jit(solution)/shard_map/slice | solution.py:267
  55.3 3.7 %copy-start.16 = (s32[32]{0:T(128)S(1)}, s32[32]{0:T(128)}, u32[]{:S(2)}) copy-start(s32[32]{0:T(128)} %fusion.108) | copy-start | bytes 388
  55.7 3.8 %copy-start.10 = (bf16[8,6,256]{2,1,0:T(8,128)(2,1)S(1)}, bf16[8,6,256]{2,1,0:T(8,128)(2,1)}, u32[]{:S(2)}) copy-start(bf16[8,6,256]{2,1,0:T(8,128)(2,1)} %copy-done.9) | copy-start | bytes 73732
  55.7 4.5 %copy-start.13 = (s32[6]{0:T(128)S(1)}, s32[6]{0:T(128)}, u32[]{:S(2)}) copy-start(s32[6]{0:T(128)} %copy-done.12) | copy-start | bytes 76
  56.6 27.9 %copy-start.2 = (bf16[8,12,256]{2,0,1:T(8,128)(2,1)}, bf16[8,12,256]{2,0,1:T(8,128)(2,1)S(1)}, u32[]{:S(2)}) copy-start(bf16[8,12,256]{2,0,1:T(8,128)(2,1)S(1)} %fusion.37) | copy-start | bytes 147460
  56.9 3.1 %collective-permute-start.2 = (bf16[8,3584]{1,0:T(8,128)(2,1)S(1)}, bf16[8,3584]{1,0:T(8,128)(2,1)S(1)}, u32[]{:S(2)}, u32[]{:S(2)}) collective-permute-start(bf16[8,3584]{1,0:T(8,128)(2,1)S(1)} %pad_maximum_fusion.5), channel_id=1, source_target_pairs={{0,16},{16,0},{32,48},{48,32},{64,80},{80,64},{96,112},{112,96},{1... | collective-permute-start | bytes 172040 | tf_op jit(solution)/shard_map/ppermute | solution.py:28
  86.6 2.7 %copy-start.6 = (bf16[8,8,256]{2,0,1:T(8,128)(2,1)S(1)}, bf16[8,8,256]{2,0,1:T(8,128)(2,1)}, u32[]{:S(2)}) copy-start(bf16[8,8,256]{2,0,1:T(8,128)(2,1)} %copy-done.5) | copy-start | bytes 98308
  86.6 2.7 %copy-start.14 = (s32[6]{0:T(128)S(1)}, s32[6]{0:T(128)}, u32[]{:S(2)}) copy-start(s32[6]{0:T(128)} %copy-done.12) | copy-start | bytes 76

commit v9 on v6

--- a/solution.py
+++ b/solution.py
@@ -192,20 +192,13 @@
     per_owner = per_dev * 3 // 4
     parity = tile_group % 2
 
-    both_states = jnp.concatenate([atmos_state, ocean_state], axis=1)
-    edges_cm = pick(edge_matrix(), both_states, "qe,bcq->cbe")
-    tables = lax.dynamic_slice_in_dim(
-        jnp.concatenate([neighbours, rotations, sea_mask[:, None]], axis=1), first_tile, per_dev, 0
-    )
-    sea_here = tables[:, 8].astype(jnp.bfloat16)
-    edges_cm = jnp.concatenate(
-        [edges_cm[:atmos_local], edges_cm[atmos_local:] * sea_here[None, :, None]], axis=0
-    )
-    edge_flat = edges_cm.reshape(-1)
-    edge_size = edge_flat.shape[0]
-    outgoing = jnp.concatenate([edge_flat, ocean_state.reshape(-1)])
+    outgoing = jnp.concatenate(
+        [atmos_state.reshape(-1, pixels), ocean_state.reshape(-1, pixels)], axis=0
+    )
     from_left = lax.ppermute(outgoing, "tiles", [(i, (i + 1) % groups) for i in range(groups)])
     from_right = lax.ppermute(outgoing, "tiles", [((i + 1) % groups, i) for i in range(groups)])
+    atmos_rows = per_dev * atmos_local
+    tables = lax.dynamic_slice_in_dim(jnp.concatenate([neighbours, rotations], axis=1), first_tile, per_dev, 0)
 
     pair_tiles = 2 * per_dev
     pair_first = tile_group // 2 * pair_tiles
@@ -223,6 +216,7 @@
 
     adjacent = tables[:, :4]
     turn_codes = tables[:, 4:8]
+    rim_mask = sea_mask[adjacent].astype(jnp.bfloat16).reshape(-1)
     local_adjacent = (adjacent // per_dev - tile_group + 1) % groups * per_dev + adjacent % per_dev
     tile_hit = local_adjacent[None, None, :, :] == jnp.arange(3 * per_dev, dtype=jnp.int32)[
         :, None, None, None
@@ -236,23 +230,28 @@
         == SIDE - 1 - lax.broadcasted_iota(jnp.int32, (SIDE, SIDE), 1)
     ).astype(jnp.bfloat16)
 
-    partner_state = jnp.where(parity == 0, from_right[edge_size:], from_left[edge_size:])
+    partner_state = jnp.where(parity == 0, from_right[atmos_rows:], from_left[atmos_rows:])
     pair_state = pair_order(ocean_state, partner_state.reshape(ocean_state.shape), parity)
     ocean_cm = pick(own_pick, pair_state, "st,tcp->csp")
     own_ocean = pick(own_pick, pair_state, "st,tcp->scp")
 
+    edge_pick = edge_matrix()
+    wide_atmos = jnp.concatenate(
+        [from_left[:atmos_rows], atmos_state.reshape(-1, pixels), from_right[:atmos_rows]], axis=0
+    ).reshape(3 * per_dev, atmos_local, pixels)
+    wide_ocean = jnp.concatenate(
+        [from_left[atmos_rows:], ocean_state.reshape(-1, pixels), from_right[atmos_rows:]], axis=0
+    ).reshape(3 * per_dev, ocean_local, pixels)
     widened = jnp.concatenate(
-        [
-            from_left[:edge_size].reshape(edges_cm.shape),
-            edges_cm,
-            from_right[:edge_size].reshape(edges_cm.shape),
-        ],
-        axis=1,
+        [pick(edge_pick, wide_atmos, "qe,bcq->cbe"), pick(edge_pick, wide_ocean, "qe,bcq->cbe")], axis=0
     ).reshape(chans, 3 * per_dev * 4, SIDE)
     straight = pick(rim_pick, widened, "xy,cxk->cyk")
     turned = pick(flip, straight, "kj,cyk->cyj")
     reverse = (turn_codes >= 4).reshape(-1)
-    rims_cm = jnp.where(reverse[None, :, None], turned, straight).reshape(chans, per_dev, 4 * SIDE)
+    rims_cm = jnp.where(reverse[None, :, None], turned, straight)
+    rims_cm = jnp.concatenate(
+        [rims_cm[:atmos_local], rims_cm[atmos_local:] * rim_mask[None, :, None]], axis=0
+    ).reshape(chans, per_dev, 4 * SIDE)
 
     early = 2 * SIDE
     atmos_int, atmos_rims, ocean_head = gather_rows(

time: 88.1 us -> 88.3 us (level)
  other arithmetic: 2.95 us -> 4.91 us
  local copies, waits for them, and re-layouts: 15.5 us -> 14.1 us
    unnamed x31 -> x41, local copies, waits for them, and re-layouts: 4.68 us -> 3.07 us
    add x3, other arithmetic: 0.53 us -> 1.74 us  [interior_spots(): return (pixel // SIDE + 1) * (SIDE + 2) + pixel % SIDE + 1]
    pad x1, local copies, waits for them, and re-layouts: 0.91 us -> 0.02 us  [conv_cm(): weight = jnp.pad(weight, ((0, 0), (0, rows - out_chans), (0, 0)))]
    dot_general x7 -> x8, matrix products: 2.25 us -> 1.75 us  [pick(): jnp.einsum(spec, selector, values, preferred_element_type=jnp.float32)]
  transfers between devices with their start and end apart: 3 -> 3, of which waited for: 2 -> 1; matrix products, arithmetic and copies ran while one was open for 6% -> 7% of each run, Pallas kernels for 0% -> 0%
where the time goes in v9:
time: 88.3 us; the launch traced here: 87.6 us
  blocking collectives  47.9 us (54%)
  local copies, waits for them, and re-layouts  14.1 us (16%)
  starting transfers between devices  10.9 us (12%)
  matrix products  7.92 us (9%)
  other arithmetic  4.91 us (6%)
  between operations  1.31 us (1%)
    all_gather x2, blocking collectives, gather_rows(): gathered = lax.all_gather(rows, 'chan', axis=0, tiled=False)  47.9 us
    ppermute x1, starting transfers between devices, local(): lax.ppermute(outgoing, 'tiles', [((i + 1) % groups, i) for i in range(gro...  8.93 us
    dot_general x2, matrix products, conv_cm(): jnp.einsum('kc,bcp->bkp', weight.reshape(taps * rows, in_chans), padded,...  3.93 us
    reshape x6, local copies, waits for them, and re-layouts, gather_rows(): parts.append(part.reshape((groups * piece.shape[0],) + piece.shape[1:]))  3.54 us
    unnamed x41, local copies, waits for them, and re-layouts  3.07 us
    dot_general x3, matrix products, placed(): jnp.einsum('cbq,qp->bcp', piece, place_matrix(spots, width), preferred_el...  2.04 us
    slice x1, local copies, waits for them, and re-layouts, conv_cm(): term = products[:, tap_index, :out_chans, offset:offset + out_span]  1.99 us
    ppermute x1, starting transfers between devices, partner(): return lax.ppermute(value, axis, pairs)  1.92 us
  transfers between devices with their start and end apart: 3, of which 1 were waited for; matrix products, arithmetic and copies ran while one was open for 7% of the time, Pallas kernels for 0%

profile of v9, /device:TPU:6, one launch (start us, length us, event | category | flops | bytes accessed | tf_op | source)
XLA Modules:
  0.0 87.6 jit_solution(10575924297362834955)
XLA Ops:
  0.7 0.9 copy.196
  1.6 0.8 pad_maximum_fusion.3
  2.3 8.9 %collective-permute-start.1 = (bf16[160,256]{1,0:T(8,128)(2,1)S(1)}, bf16[160,256]{1,0:T(8,128)(2,1)S(1)}, u32[]{:S(2)}, u32[]{:S(2)}) collective-permute-start(bf16[160,256]{1,0:T(8,128)(2,1)S(1)} %pad_maximum_fusion.3), channel_id=1, source_target_pairs={{16,0},{32,16},{48,32},{64,48},{80,64},{96,80},{112,96},{128,112},... | collective-permute-start | bytes 245768 | tf_op jit(solution)/shard_map/ppermute | solution.py:199
  11.3 0.6 fusion.108
  11.9 0.6 fusion.106
  12.5 0.6 fusion.102
  13.0 0.8 fusion.80
  13.9 0.8 dynamic_slice.7
  15.1 0.7 gather_fusion
  19.3 24.7 %all_gather.6 = bf16[16,126,256]{2,1,0:T(8,128)(2,1)S(1)} all-gather(bf16[1,126,256]{2,1,0:T(8,128)(2,1)S(1)} %all_gather_reshape.6), channel_id=1, replica_groups=mesh['tiles'=32,'chan'=16] {'chan'}, dimensions={0}, use_global_device_ids=true | all-gather | bytes 1096704 | tf_op jit(solution)/shard_map/all_gather | solution.py:94
  44.1 0.6 copy.262
  45.0 0.7 reshape.274
  46.1 1.1 %reshape.267 = bf16[192,8,64]{2,1,0:T(8,128)(2,1)} reshape(bf16[16,6144]{1,0:T(8,128)(2,1)S(1)} %slice.170) | data formatting | bytes 393216 | tf_op jit(solution)/shard_map/reshape | solution.py:102
  47.4 1.3 %fusion.14 = f32[326,192,8]{0,1,2:T(8,128)S(1)} fusion(bf16[192,8,256]{2,1,0:T(8,128)(2,1)S(1)} %reshape.266, s32[256]{0:T(256)} %fusion.102), kind=kOutput, calls=%fused_computation.27 | convolution fusion | flops 256460288 | bytes 2790400 | tf_op jit(solution)/shard_map/cbq,qp->bcp/dot_general | solution.py:127
  48.7 3.2 %fusion.1 = f32[8,326,144]{1,2,0:T(8,128)} fusion(bf16[144,192,1]{1,0,2:T(8,128)(2,1)S(1)} %bitcast.179, f32[326,192,8]{0,1,2:T(8,128)S(1)} %fusion.14, bf16[192,8,64]{2,1,0:T(8,128)(2,1)} %reshape.267, s32[64]{0:T(128)S(1)} %pad_add_fusion.1), kind=kOutput, calls=%fused_computation.3 | convolution fusion | flops 209328512 | bytes 3757312 | tf_op jit(solution)/shard_map/kc,bcp->bkp/dot_general | solution.py:141
  51.9 2.0 %fusion.113 = (f32[8,1,12,288]{3,2,1,0:T(8,128)S(1)}, f32[8,1,12,288]{3,2,1,0:T(8,128)S(1)}, f32[8,1,12,288]{3,2,1,0:T(8,128)S(1)}, f32[8,1,12,288]{3,2,1,0:T(8,...) fusion(f32[8,9,16,326]{3,2,1,0:T(8,128)} %bitcast.162), kind=kLoop, calls=%fused_computation.200 | loop fusion | bytes 1990656 | tf_op jit(solution)/shard_map/slice | solution.py:150
  55.2 1.9 %collective-permute-start.2 = (bf16[8,3584]{1,0:T(8,128)(2,1)S(1)}, bf16[8,3584]{1,0:T(8,128)(2,1)S(1)}, u32[]{:S(2)}, u32[]{:S(2)}) collective-permute-start(bf16[8,3584]{1,0:T(8,128)(2,1)S(1)} %pad_maximum_fusion.7), channel_id=1, source_target_pairs={{0,16},{16,0},{32,48},{48,32},{64,80},{80,64},{96,112},{112,96},{1... | collective-permute-start | bytes 172040 | tf_op jit(solution)/shard_map/ppermute | solution.py:28
  57.8 0.6 collective-permute-done.2
  59.1 23.1 %all_gather.7 = bf16[16,126,256]{2,1,0:T(8,128)(2,1)S(1)} all-gather(bf16[1,126,256]{2,1,0:T(8,128)(2,1)S(1)} %all_gather_reshape.7), channel_id=1, replica_groups=mesh['tiles'=32,'chan'=16] {'chan'}, dimensions={0}, use_global_device_ids=true | all-gather | bytes 1096704 | tf_op jit(solution)/shard_map/all_gather | solution.py:94
  82.2 0.6 copy.263
  83.1 0.8 reshape.280
  84.2 0.7 convolution_bitcast_fusion
  85.2 0.9 %reshape.285 = bf16[192,6,256]{2,1,0:T(8,128)(2,1)S(1)} reshape(bf16[16,18432]{1,0:T(8,128)(2,1)S(1)} %slice.196) | data formatting | bytes 1179648 | tf_op jit(solution)/shard_map/reshape | solution.py:102
  87.0 0.6 copy.238
  (125 shorter events, 8.9 us)
Async XLA Ops:
  0.6 83.6 %copy-start = (bf16[9,8,128]{2,1,0:T(8,128)(2,1)S(1)}, bf16[9,8,128]{2,1,0:T(8,128)(2,1)}, u32[]{:S(2)}) copy-start(bf16[9,8,128]{2,1,0:T(8,128)(2,1)} %param.11) | copy-start | bytes 55300
  0.6 15.5 %copy-start.2 = (bf16[8,12,256]{2,0,1:T(8,128)(2,1)S(1)}, bf16[8,12,256]{2,0,1:T(8,128)(2,1)}, u32[]{:S(2)}) copy-start(bf16[8,12,256]{2,0,1:T(8,128)(2,1)} %param.8) | copy-start | bytes 147460
  0.7 14.4 %copy-start.1 = (s32[256]{0:T(256)S(1)}, s32[256]{0:T(256)}, u32[]{:S(2)}) copy-start(s32[256]{0:T(256)} %param.13) | copy-start | bytes 3076
  2.3 14.4 %copy-start.6 = (bf16[9,12,192]{2,1,0:T(8,128)(2,1)S(1)}, bf16[9,12,192]{2,1,0:T(8,128)(2,1)}, u32[]{:S(2)}) copy-start(bf16[9,12,192]{2,1,0:T(8,128)(2,1)} %param.10) | copy-start | bytes 124420
  2.3 14.6 %collective-permute-start.1 = (bf16[160,256]{1,0:T(8,128)(2,1)S(1)}, bf16[160,256]{1,0:T(8,128)(2,1)S(1)}, u32[]{:S(2)}, u32[]{:S(2)}) collective-permute-start(bf16[160,256]{1,0:T(8,128)(2,1)S(1)} %pad_maximum_fusion.3), channel_id=1, source_target_pairs={{16,0},{32,16},{48,32},{64,48},{80,64},{96,80},{112,96},{128,112},... | collective-permute-start | bytes 245768 | tf_op jit(solution)/shard_map/ppermute | solution.py:199
  11.3 5.7 %collective-permute-start = (bf16[160,256]{1,0:T(8,128)(2,1)S(1)}, bf16[160,256]{1,0:T(8,128)(2,1)S(1)}, u32[]{:S(2)}, u32[]{:S(2)}) collective-permute-start(bf16[160,256]{1,0:T(8,128)(2,1)S(1)} %pad_maximum_fusion.3), channel_id=1, source_target_pairs={{0,16},{16,32},{32,48},{48,64},{64,80},{80,96},{96,112},{112,128},... | collective-permute-start | bytes 245768 | tf_op jit(solution)/shard_map/ppermute | solution.py:198
  15.1 2.0 %copy-start.4 = (bf16[8,8,256]{2,1,0:T(8,128)(2,1)S(1)}, bf16[8,8,256]{2,1,0:T(8,128)(2,1)}, u32[]{:S(2)}) copy-start(bf16[8,8,256]{2,1,0:T(8,128)(2,1)} %param.9) | copy-start | bytes 98308
  16.8 1.1 %copy-start.14 = (s32[6]{0:T(128)}, s32[6]{0:T(128)S(1)}, u32[]{:S(2)}) copy-start(s32[6]{0:T(128)S(1)} %convert_reduce_fusion) | copy-start | bytes 76
  17.6 0.6 copy-start.9
  17.6 0.6 copy-start.11
  17.8 26.8 %copy-start.7 = (bf16[8,6,256]{2,1,0:T(8,128)(2,1)}, bf16[8,6,256]{2,1,0:T(8,128)(2,1)S(1)}, u32[]{:S(2)}) copy-start(bf16[8,6,256]{2,1,0:T(8,128)(2,1)S(1)} %fusion.12) | copy-start | bytes 73732
  53.9 1.3 %copy-start.5 = (bf16[8,512]{1,0:T(8,128)(2,1)S(1)}, bf16[8,512]{1,0:T(8,128)(2,1)}, u32[]{:S(2)}) copy-start(bf16[8,512]{1,0:T(8,128)(2,1)} %reshape.274) | copy-start | bytes 24580
  53.9 3.2 %copy-start.16 = (s32[32]{0:T(128)S(1)}, s32[32]{0:T(128)}, u32[]{:S(2)}) copy-start(s32[32]{0:T(128)} %fusion.108) | copy-start | bytes 388
  53.9 3.7 %copy-start.8 = (bf16[8,6,256]{2,1,0:T(8,128)(2,1)S(1)}, bf16[8,6,256]{2,1,0:T(8,128)(2,1)}, u32[]{:S(2)}) copy-start(bf16[8,6,256]{2,1,0:T(8,128)(2,1)} %copy-done.7) | copy-start | bytes 73732
  54.3 4.1 %copy-start.15 = (s32[6]{0:T(128)S(1)}, s32[6]{0:T(128)}, u32[]{:S(2)}) copy-start(s32[6]{0:T(128)} %copy-done.14) | copy-start | bytes 76
  55.1 27.6 %copy-start.3 = (bf16[8,12,256]{2,0,1:T(8,128)(2,1)}, bf16[8,12,256]{2,0,1:T(8,128)(2,1)S(1)}, u32[]{:S(2)}) copy-start(bf16[8,12,256]{2,0,1:T(8,128)(2,1)S(1)} %fusion.40) | copy-start | bytes 147460
  55.2 3.1 %collective-permute-start.2 = (bf16[8,3584]{1,0:T(8,128)(2,1)S(1)}, bf16[8,3584]{1,0:T(8,128)(2,1)S(1)}, u32[]{:S(2)}, u32[]{:S(2)}) collective-permute-start(bf16[8,3584]{1,0:T(8,128)(2,1)S(1)} %pad_maximum_fusion.7), channel_id=1, source_target_pairs={{0,16},{16,0},{32,48},{48,32},{64,80},{80,64},{96,112},{112,96},{1... | collective-permute-start | bytes 172040 | tf_op jit(solution)/shard_map/ppermute | solution.py:28
  82.2 1.7 %copy-start.13 = (s32[224]{0:T(256)S(1)}, s32[224]{0:T(256)}, u32[]{:S(2)}) copy-start(s32[224]{0:T(256)} %fusion.106) | copy-start | bytes 2692
  84.2 2.3 %copy-start.17 = (bf16[8,192]{1,0:T(8,128)(2,1)S(1)}, bf16[8,192]{1,0:T(8,128)(2,1)}, u32[]{:S(2)}) copy-start(bf16[8,192]{1,0:T(8,128)(2,1)} %param.12) | copy-start | bytes 9220
  84.2 2.5 %copy-start.10 = (bf16[8,8,256]{2,0,1:T(8,128)(2,1)S(1)}, bf16[8,8,256]{2,0,1:T(8,128)(2,1)}, u32[]{:S(2)}) copy-start(bf16[8,8,256]{2,0,1:T(8,128)(2,1)} %copy-done.9) | copy-start | bytes 98308
  84.2 2.5 %copy-start.12 = (bf16[8,8,256]{2,0,1:T(8,128)(2,1)S(1)}, bf16[8,8,256]{2,0,1:T(8,128)(2,1)}, u32[]{:S(2)}) copy-start(bf16[8,8,256]{2,0,1:T(8,128)(2,1)} %copy-done.11) | copy-start | bytes 98308
